TPU v7x, 256 devices: a whole 4x4x8 slice. The times are simulated.
256 devices in a mesh: space: 32 (over x, z), member: 4 (over y), lag: 2 (over core).
Axes of the slice: x: 4, y: 4, z: 8, core: 2. Of those that a mesh axis runs over, the one named last changes fastest.
Arguments:
- anomalies: bfloat16 [2, 131072, 512], P('lag', 'space', 'member'), may hold values from -6 to 6
- mean_state: float32 [2, 131072], P('lag', 'space'), may hold values from -6 to 6
- footprints: bfloat16 [4, 2, 128, 256, 512], P(None, 'lag', 'space'), may hold values from -0.03125 to 0.03125
- slot_tiles: int32 [4, 2, 128], P(None, 'lag', 'space'), may hold values from 0 to 7, as said below
- slot_counts: int32 [4, 2, 32], P(None, 'lag', 'space'), may hold values from 0 to 4, as said below
- obs_values: float32 [32, 4, 256], P('space'), may hold values from -6 to 6
- obs_errors: float32 [32, 4, 256], P('space'), may hold values from 0.5 to 1.5
- owners: int32 [4], replicated, may hold values from 0 to 31
- batch_order: int32 [4], replicated, may hold values from 0 to 3, as said below
Outputs:
- analysis_anoms: bfloat16 [2, 131072, 512], P('lag', 'space', 'member')
- analysis_mean: float32 [2, 131072], P('lag', 'space')
Inputs may be any that keep to these rules, and one draw needn't show every extreme that they name: `slot_counts`: in every batch some lag week and space group has exactly 4 live slots. `slot_tiles`: within one batch, lag week and space group the 4 slots name distinct local tiles. `batch_order`: A permutation.
All inputs are finite; a program needn't handle non-finite values.
Results may differ from a plain program's by a relative error of at most 0.008.
Values may be sent and summed in bfloat16 or wider, within the bound.
No kernel may reach another device: no remote copies, remote signals or barrier semaphores. Data moves between devices by JAX's collectives and lax.ppermute only.
A program may use at most 64 MiB of HBM per device.

v0:
```python
import jax
import jax.numpy as jnp
from jax import lax
from jax.sharding import PartitionSpec as P


def spread(array, axis, root):
    mine = lax.axis_index(axis) == root
    return lax.psum(jnp.where(mine, array, jnp.zeros_like(array)), axis)


def innovation(obs_round, values_now, obs_means, errors_now, members):
    obs_total = obs_round.shape[0]
    innov_cov = jnp.dot(obs_round, obs_round.T, preferred_element_type=jnp.float32) / (
        members - 1
    ) + jnp.diag(errors_now * errors_now)
    factor = jnp.linalg.cholesky(innov_cov)
    identity = jnp.eye(obs_total, dtype=jnp.float32)
    inverse_sum = lax.linalg.triangular_solve(
        factor + jnp.diag(errors_now), identity, left_side=True, lower=True
    )
    transform = lax.linalg.triangular_solve(
        factor, inverse_sum, left_side=True, lower=True, transpose_a=True
    )
    forward = lax.linalg.triangular_solve(
        factor, (values_now - obs_means)[:, None], left_side=True, lower=True
    )
    weights_obs = lax.linalg.triangular_solve(
        factor, forward, left_side=True, lower=True, transpose_a=True
    )[:, 0]
    return (transform, weights_obs)


def body(
    anomalies,
    mean_state,
    footprints,
    slot_tiles,
    slot_counts,
    obs_values,
    obs_errors,
    owners,
    batch_order,
):
    highest = lax.Precision.HIGHEST
    batches = footprints.shape[0]
    slot_dev = footprints.shape[2]
    tile_cells = footprints.shape[4]
    member_dev = anomalies.shape[2]
    groups = lax.axis_size("member")
    members = member_dev * groups
    tile_anoms = anomalies[0].reshape(-1, tile_cells, member_dev)
    tile_means = mean_state[0].reshape(-1, tile_cells)
    for position in range(batches):
        batch_now = batch_order[position]
        values_now, errors_now = (
            spread(obs_values[0, batch_now], "space", owners[batch_now]),
            spread(obs_errors[0, batch_now], "space", owners[batch_now]),
        )
        tile_ids = slot_tiles[batch_now, 0]
        live_count = slot_counts[batch_now, 0, 0]
        live_mask = jnp.arange(slot_dev) < live_count
        slot_anoms = tile_anoms[tile_ids]
        slot_means = tile_means[tile_ids]
        prints = footprints[batch_now, 0]
        mean_round = slot_means.astype(jnp.bfloat16)
        masked = jnp.where(live_mask[:, None, None], slot_anoms, 0)
        part_anoms = jnp.einsum("spt,stm->pm", prints, masked, preferred_element_type=jnp.float32)
        masked_mean = jnp.where(live_mask[:, None], mean_round, 0)
        part_means = jnp.einsum(
            "spt,st->p", prints, masked_mean, preferred_element_type=jnp.float32
        )
        obs_anoms, obs_means = lax.psum((part_anoms, part_means), ("space", "lag"))
        own_round = obs_anoms.astype(jnp.bfloat16)
        obs_round = lax.all_gather(own_round, "member", axis=1, tiled=True)
        transform, weights_obs = innovation(obs_round, values_now, obs_means, errors_now, members)
        all_anoms = lax.all_gather(slot_anoms, "member", axis=2, tiled=True)
        covariance = jnp.einsum(
            "stm,pm->stp", all_anoms, obs_round, preferred_element_type=jnp.float32
        )
        gain_tile = (
            jnp.einsum("stp,pq->stq", covariance, transform, precision=highest) / (members - 1)
        ).astype(jnp.bfloat16)
        shift_mean = jnp.einsum("stp,p->st", covariance, weights_obs, precision=highest) / (
            members - 1
        )
        step_anoms = jnp.einsum(
            "stp,pm->stm", gain_tile, own_round, preferred_element_type=jnp.float32
        )
        updated = (slot_anoms.astype(jnp.float32) - step_anoms).astype(jnp.bfloat16)
        tile_anoms = tile_anoms.at[tile_ids].set(
            jnp.where(live_mask[:, None, None], updated, slot_anoms)
        )
        tile_means = tile_means.at[tile_ids].set(
            jnp.where(live_mask[:, None], slot_means + shift_mean, slot_means)
        )
    return (tile_anoms.reshape(1, -1, member_dev), tile_means.reshape(1, -1))


def solution(mesh):
    return jax.shard_map(
        body,
        mesh=mesh,
        in_specs=(
            P("lag", "space", "member"),
            P("lag", "space"),
            P(None, "lag", "space", None, None),
            P(None, "lag", "space"),
            P(None, "lag", "space"),
            P("space", None, None),
            P("space", None, None),
            P(),
            P(),
        ),
        out_specs=(P("lag", "space", "member"), P("lag", "space")),
        check_vma=False,
    )
```

profile of v0, /device:TPU:1, one launch (start us, length us, event | category | flops | bytes accessed | tf_op | source)
XLA Modules:
  0.0 1575.1 jit_solution(11899528764224446075)
XLA Ops:
  25.2 249.5 %all-reduce.10 = (bf16[256,128]{1,0:T(8,128)(2,1)S(1)}, f32[256]{0:T(256)S(1)}) all-reduce(f32[256,128]{1,0:T(8,128)S(1)} %convolution_bitcast_fusion.3, f32[256]{0:T(256)S(1)} %bitcast.585), channel_id=1, replica_groups=mesh['space'=32,'member'=4,'lag'=2] {'space','lag'}, use_global_device_ids=true, to_apply=%region_0.1 | all-reduce | flops 33024 | bytes 198656 | tf_op jit(solution)/shard_map/psum | solution.py:73
  274.7 9.6 all_gather.25
  287.4 62.6 %all-reduce.5 = (f32[256]{0:T(256)S(1)}, f32[256]{0:T(256)S(1)}, f32[256]{0:T(256)S(1)}, f32[256]{0:T(256)}, f32[256]{0:T(256)S(1)}, /*index=5*/f32[256]{0:T(256)}, f32[256]{0:T(256)S(1)}, f32[256]{0:T(256)}) all-reduce(f32[256]{0:T(256)S(1)} %bitcast.599, ...), channel_id=1, replica_groups=mesh['space'=32,'member'=4,'lag'=2] {'space'}, use_global_device_ids=true, to_apply=%region_1.2 | all-reduce | flops 2048 | bytes 16384 | tf_op jit(solution)/shard_map/psum | solution.py:9
  350.5 11.7 cholesky.214
  362.3 9.8 custom-call.35
  372.7 11.7 cholesky.231
  391.4 4.4 while.33
  400.0 19.8 %custom-call.36 = f32[2,128,128]{1,2,0:T(8,128)S(1)} custom-call(f32[2,128,128]{2,1,0:T(8,128)S(1)} %get-tuple-element.111), custom_call_target="InvertDiagBlocksLowerTriangular" | custom-call | tf_op jit(solution)/shard_map/triangular_solve/custom-call.0 | solution.py:19
  419.9 19.7 %custom-call.37 = f32[2,128,128]{1,2,0:T(8,128)S(1)} custom-call(f32[2,128,128]{2,1,0:T(8,128)S(1)} %get-tuple-element.112), custom_call_target="InvertDiagBlocksLowerTriangular" | custom-call | tf_op jit(solution)/shard_map/triangular_solve/custom-call.4 | solution.py:22
  464.9 257.4 %all-reduce.11 = (bf16[256,128]{1,0:T(8,128)(2,1)S(1)}, f32[256]{0:T(256)S(1)}) all-reduce(f32[256,128]{1,0:T(8,128)S(1)} %convolution_bitcast_fusion.2, f32[256]{0:T(256)S(1)} %bitcast.582), channel_id=1, replica_groups=mesh['space'=32,'member'=4,'lag'=2] {'space','lag'}, use_global_device_ids=true, to_apply=%region_7.11 | all-reduce | flops 33024 | bytes 198656 | tf_op jit(solution)/shard_map/psum | solution.py:73
  722.9 9.1 all_gather.27
  733.9 11.7 cholesky.248
  745.7 9.8 custom-call.38
  756.1 11.7 cholesky.265
  770.7 4.6 while.34
  779.6 19.7 %custom-call.39 = f32[2,128,128]{1,2,0:T(8,128)S(1)} custom-call(f32[2,128,128]{2,1,0:T(8,128)S(1)} %get-tuple-element.113), custom_call_target="InvertDiagBlocksLowerTriangular" | custom-call | tf_op jit(solution)/shard_map/triangular_solve/custom-call.0 | solution.py:19
  799.3 19.7 %custom-call.40 = f32[2,128,128]{1,2,0:T(8,128)S(1)} custom-call(f32[2,128,128]{2,1,0:T(8,128)S(1)} %get-tuple-element.114), custom_call_target="InvertDiagBlocksLowerTriangular" | custom-call | tf_op jit(solution)/shard_map/triangular_solve/custom-call.4 | solution.py:22
  841.4 248.5 %all-reduce.12 = (bf16[256,128]{1,0:T(8,128)(2,1)S(1)}, f32[256]{0:T(256)S(1)}) all-reduce(f32[256,128]{1,0:T(8,128)S(1)} %convolution_bitcast_fusion.1, f32[256]{0:T(256)S(1)} %bitcast.583), channel_id=1, replica_groups=mesh['space'=32,'member'=4,'lag'=2] {'space','lag'}, use_global_device_ids=true, to_apply=%region_10.14 | all-reduce | flops 33024 | bytes 198656 | tf_op jit(solution)/shard_map/psum | solution.py:73
  1090.6 9.1 all_gather.29
  1101.5 11.7 cholesky.282
  1113.4 9.8 custom-call.41
  1123.8 11.7 cholesky.299
  1146.9 19.7 %custom-call.42 = f32[2,128,128]{1,2,0:T(8,128)S(1)} custom-call(f32[2,128,128]{2,1,0:T(8,128)S(1)} %get-tuple-element.115), custom_call_target="InvertDiagBlocksLowerTriangular" | custom-call | tf_op jit(solution)/shard_map/triangular_solve/custom-call.0 | solution.py:19
  1166.6 19.7 %custom-call.43 = f32[2,128,128]{1,2,0:T(8,128)S(1)} custom-call(f32[2,128,128]{2,1,0:T(8,128)S(1)} %get-tuple-element.116), custom_call_target="InvertDiagBlocksLowerTriangular" | custom-call | tf_op jit(solution)/shard_map/triangular_solve/custom-call.4 | solution.py:22
  1208.6 248.8 %all-reduce.13 = (bf16[256,128]{1,0:T(8,128)(2,1)S(1)}, f32[256]{0:T(256)S(1)}) all-reduce(f32[256,128]{1,0:T(8,128)S(1)} %convolution_bitcast_fusion, f32[256]{0:T(256)S(1)} %bitcast.584), channel_id=1, replica_groups=mesh['space'=32,'member'=4,'lag'=2] {'space','lag'}, use_global_device_ids=true, to_apply=%region_13.17 | all-reduce | flops 33024 | bytes 198656 | tf_op jit(solution)/shard_map/psum | solution.py:73
  1458.0 9.3 all_gather.31
  1469.2 11.7 cholesky.316
  1481.1 9.8 custom-call.44
  1491.5 11.7 cholesky.333
  1505.9 4.4 while.38
  1514.7 19.7 %custom-call.45 = f32[2,128,128]{1,2,0:T(8,128)S(1)} custom-call(f32[2,128,128]{2,1,0:T(8,128)S(1)} %get-tuple-element.117), custom_call_target="InvertDiagBlocksLowerTriangular" | custom-call | tf_op jit(solution)/shard_map/triangular_solve/custom-call.0 | solution.py:19
  1534.4 19.7 %custom-call.46 = f32[2,128,128]{1,2,0:T(8,128)S(1)} custom-call(f32[2,128,128]{2,1,0:T(8,128)S(1)} %get-tuple-element.118), custom_call_target="InvertDiagBlocksLowerTriangular" | custom-call | tf_op jit(solution)/shard_map/triangular_solve/custom-call.4 | solution.py:22
  (426 shorter events, 169.8 us)
Async XLA Ops:
  7.2 9.8 copy-start.55
  7.2 11.3 copy-start.32
  7.2 439.9 %all-gather.9.cloned.1.call-start = ((), (), s32[]{:S(2)}) async-start(), calls=%async_computation | async-start | bytes 2621440 | tf_op jit(solution)/shard_map/all_gather | solution.py:77
  8.5 13.8 copy-start.25
  17.0 378.9 %copy-start.44 = (s32[4]{0:T(128)}, s32[4]{0:T(128)S(1)}, u32[]{:S(2)}) copy-start(s32[4]{0:T(128)S(1)} %get-tuple-element.312) | copy-start | bytes 52
  17.0 424.3 %copy-start.42 = (s32[4]{0:T(128)}, s32[4]{0:T(128)S(1)}, u32[]{:S(2)}) copy-start(s32[4]{0:T(128)S(1)} %get-tuple-element.314) | copy-start | bytes 52
  17.0 424.9 %copy-start.40 = (s32[4]{0:T(128)}, s32[4]{0:T(128)S(1)}, u32[]{:S(2)}) copy-start(s32[4]{0:T(128)S(1)} %get-tuple-element.311) | copy-start | bytes 52
  18.4 265.9 %copy-start.33 = (s32[4]{0:T(128)S(1)}, s32[4]{0:T(128)}, u32[]{:S(2)}) copy-start(s32[4]{0:T(128)} %param.25) | copy-start | bytes 52
  18.4 268.9 %copy-start.53 = (f32[1,4,256]{2,1,0:T(4,128)S(1)}, f32[1,4,256]{2,1,0:T(4,128)}, u32[]{:S(2)}) copy-start(f32[1,4,256]{2,1,0:T(4,128)} %param.23) | copy-start | bytes 12292
  18.4 268.9 %copy-start.54 = (f32[1,4,256]{2,1,0:T(4,128)S(1)}, f32[1,4,256]{2,1,0:T(4,128)}, u32[]{:S(2)}) copy-start(f32[1,4,256]{2,1,0:T(4,128)} %param.24) | copy-start | bytes 12292
  18.5 805.2 %all-gather.11.cloned.1.call-start = ((), (), s32[]{:S(2)}) async-start(), calls=%async_computation.1 | async-start | bytes 2621440 | tf_op jit(solution)/shard_map/all_gather | solution.py:77
  19.9 5.3 copy-start.38
  23.5 251.2 %copy-start.20 = (f32[4,512]{1,0:T(4,128)}, f32[4,512]{1,0:T(4,128)S(1)}, u32[]{:S(2)}) copy-start(f32[4,512]{1,0:T(4,128)S(1)} %gather_fusion.4) | copy-start | bytes 24580
  274.7 75.3 %copy-start.12 = (bf16[256,128]{1,0:T(8,128)(2,1)}, bf16[256,128]{1,0:T(8,128)(2,1)S(1)}, u32[]{:S(2)}) copy-start(bf16[256,128]{1,0:T(8,128)(2,1)S(1)} %get-tuple-element.261) | copy-start | bytes 196612
  284.3 102.8 %copy-start.5 = (bf16[256,512]{1,0:T(8,128)(2,1)}, bf16[256,512]{1,0:T(8,128)(2,1)S(1)}, u32[]{:S(2)}) copy-start(bf16[256,512]{1,0:T(8,128)(2,1)S(1)} %all_gather.25) | copy-start | bytes 786436
  350.0 89.6 %copy-start.30 = (f32[256]{0:T(256)}, f32[256]{0:T(256)S(1)}, u32[]{:S(2)}) copy-start(f32[256]{0:T(256)S(1)} %get-tuple-element.265) | copy-start | bytes 3076
  350.0 90.2 %copy-start.28 = (f32[256]{0:T(256)}, f32[256]{0:T(256)S(1)}, u32[]{:S(2)}) copy-start(f32[256]{0:T(256)S(1)} %get-tuple-element.267) | copy-start | bytes 3076
  350.0 90.7 %copy-start.26 = (f32[256]{0:T(256)}, f32[256]{0:T(256)S(1)}, u32[]{:S(2)}) copy-start(f32[256]{0:T(256)S(1)} %get-tuple-element.269) | copy-start | bytes 3076
  395.8 24.0 %copy-start.60 = (s32[2,2]{1,0:T(2,128)}, s32[2,2]{1,0:T(2,128)S(1)}, u32[]{:S(2)}) copy-start(s32[2,2]{1,0:T(2,128)S(1)} %get-tuple-element.708) | copy-start | bytes 52
  455.9 735.0 %all-gather.13.cloned.1.call-start = ((), (), s32[]{:S(2)}) async-start(), calls=%async_computation.2 | async-start | bytes 2621440 | tf_op jit(solution)/shard_map/all_gather | solution.py:77
  722.9 47.7 %copy-start.31 = (f32[256]{0:T(256)S(1)}, f32[256]{0:T(256)}, u32[]{:S(2)}) copy-start(f32[256]{0:T(256)} %copy-done.30) | copy-start | bytes 3076
  733.7 37.0 %copy-start.61 = (s32[2,2]{1,0:T(2,128)S(1)}, s32[2,2]{1,0:T(2,128)}, u32[]{:S(2)}) copy-start(s32[2,2]{1,0:T(2,128)} %copy-done.60) | copy-start | bytes 52
  770.7 48.3 %copy-start.59 = (f32[256]{0:T(256)S(1)}, f32[256]{0:T(256)}, u32[]{:S(2)}) copy-start(f32[256]{0:T(256)} %get-tuple-element.266) | copy-start | bytes 3076
  779.6 44.0 %copy-start.62 = (s32[2,2]{1,0:T(2,128)}, s32[2,2]{1,0:T(2,128)S(1)}, u32[]{:S(2)}) copy-start(s32[2,2]{1,0:T(2,128)S(1)} %get-tuple-element.710) | copy-start | bytes 52
  832.4 725.6 %all-gather.15.cloned.1.call-start = ((), (), s32[]{:S(2)}) async-start(), calls=%async_computation.3 | async-start | bytes 2621440 | tf_op jit(solution)/shard_map/all_gather | solution.py:77
  1090.6 47.7 %copy-start.29 = (f32[256]{0:T(256)S(1)}, f32[256]{0:T(256)}, u32[]{:S(2)}) copy-start(f32[256]{0:T(256)} %copy-done.28) | copy-start | bytes 3076
  1101.3 37.0 %copy-start.63 = (s32[2,2]{1,0:T(2,128)S(1)}, s32[2,2]{1,0:T(2,128)}, u32[]{:S(2)}) copy-start(s32[2,2]{1,0:T(2,128)} %copy-done.62) | copy-start | bytes 52
  1138.3 48.0 %copy-start.58 = (f32[256]{0:T(256)S(1)}, f32[256]{0:T(256)}, u32[]{:S(2)}) copy-start(f32[256]{0:T(256)} %get-tuple-element.268) | copy-start | bytes 3076
  1146.9 43.9 %copy-start.64 = (s32[2,2]{1,0:T(2,128)}, s32[2,2]{1,0:T(2,128)S(1)}, u32[]{:S(2)}) copy-start(s32[2,2]{1,0:T(2,128)S(1)} %get-tuple-element.712) | copy-start | bytes 52
  1458.0 47.8 %copy-start.27 = (f32[256]{0:T(256)S(1)}, f32[256]{0:T(256)}, u32[]{:S(2)}) copy-start(f32[256]{0:T(256)} %copy-done.26) | copy-start | bytes 3076
  1469.0 36.9 %copy-start.65 = (s32[2,2]{1,0:T(2,128)S(1)}, s32[2,2]{1,0:T(2,128)}, u32[]{:S(2)}) copy-start(s32[2,2]{1,0:T(2,128)} %copy-done.64) | copy-start | bytes 52
  1505.9 48.2 %copy-start.57 = (f32[256]{0:T(256)S(1)}, f32[256]{0:T(256)}, u32[]{:S(2)}) copy-start(f32[256]{0:T(256)} %get-tuple-element.270) | copy-start | bytes 3076
  (38 other events, 65.6 us)
Sparse Core Ops, SparseCore 0:
  18.6 38.9 all-gather.8
  456.0 45.4 all-gather.10
  832.5 35.6 all-gather.12
  1199.7 35.6 all-gather.14
where the time goes:
time: 1590 us; the launch traced here: 1580 us
  blocking collectives  1100 us (69%)
  other arithmetic  311 us (20%)
  matrix products  67.6 us (4%)
  local copies, waits for them, and re-layouts  60.6 us (4%)
  between operations  30.5 us (2%)
    psum x4, blocking collectives, body(): obs_anoms, obs_means = lax.psum((part_anoms, part_means), ('space', 'lag'))  1000 us
    another operation x28, other arithmetic, innovation(): factor = jnp.linalg.cholesky(innov_cov)  138 us
    another operation x9, other arithmetic, innovation(): lax.linalg.triangular_solve(factor, inverse_sum, left_side=True, lower=Tr...  78.9 us
    another operation x4, other arithmetic, innovation(): lax.linalg.triangular_solve(factor + jnp.diag(errors_now), identity, left...  78.8 us
    psum x1, blocking collectives, spread(): return lax.psum(jnp.where(mine, array, jnp.zeros_like(array)), axis)  62.6 us
    all_gather x4, blocking collectives, body(): obs_round = lax.all_gather(own_round, 'member', axis=1, tiled=True)  37.3 us
  transfers between devices with their start and end apart: 4, of which 0 were waited for; matrix products, arithmetic and copies ran while one was open for 25% of the time, Pallas kernels for 0%

commit v1 on v0

--- a/solution.py
+++ b/solution.py
@@ -51,12 +51,15 @@
     members = member_dev * groups
     tile_anoms = anomalies[0].reshape(-1, tile_cells, member_dev)
     tile_means = mean_state[0].reshape(-1, tile_cells)
+    me_member = lax.axis_index("member")
+    me_space = lax.axis_index("space")
+    me_lag = lax.axis_index("lag")
+    lead = (me_member == 0) & (me_lag == 0)
     for position in range(batches):
         batch_now = batch_order[position]
-        values_now, errors_now = (
-            spread(obs_values[0, batch_now], "space", owners[batch_now]),
-            spread(obs_errors[0, batch_now], "space", owners[batch_now]),
-        )
+        owner_here = lead & (me_space == owners[batch_now])
+        own_values = jnp.where(owner_here, obs_values[0, batch_now], 0)
+        own_errors = jnp.where(owner_here, obs_errors[0, batch_now], 0)
         tile_ids = slot_tiles[batch_now, 0]
         live_count = slot_counts[batch_now, 0, 0]
         live_mask = jnp.arange(slot_dev) < live_count
@@ -70,9 +73,15 @@
         part_means = jnp.einsum(
             "spt,st->p", prints, masked_mean, preferred_element_type=jnp.float32
         )
-        obs_anoms, obs_means = lax.psum((part_anoms, part_means), ("space", "lag"))
-        own_round = obs_anoms.astype(jnp.bfloat16)
-        obs_round = lax.all_gather(own_round, "member", axis=1, tiled=True)
+        slotted = jnp.zeros((groups,) + part_anoms.shape, jnp.float32)
+        slotted = lax.dynamic_update_index_in_dim(slotted, part_anoms, me_member, 0)
+        part_means = jnp.where(me_member == 0, part_means, 0)
+        all_anoms_obs, obs_means, values_now, errors_now = lax.psum(
+            (slotted, part_means, own_values, own_errors), ("space", "member", "lag")
+        )
+        all_round = all_anoms_obs.astype(jnp.bfloat16)
+        own_round = lax.dynamic_index_in_dim(all_round, me_member, 0, keepdims=False)
+        obs_round = jnp.transpose(all_round, (1, 0, 2)).reshape(all_round.shape[1], -1)
         transform, weights_obs = innovation(obs_round, values_now, obs_means, errors_now, members)
         all_anoms = lax.all_gather(slot_anoms, "member", axis=2, tiled=True)
         covariance = jnp.einsum(

time: 1590 us -> 802 us (0.50)
  blocking collectives: 1100 us -> 323 us
    psum x5 -> x4, blocking collectives: 1070 us -> 323 us  [body(): lax.psum((slotted, part_means, own_values, own_errors), ('space', 'member...]
    all_gather x4 -> x0, blocking collectives: 37.3 us -> none  [body(): obs_round = lax.all_gather(own_round, 'member', axis=1, tiled=True)]
  transfers between devices with their start and end apart: 4 -> 4, of which waited for: 0 -> 0; matrix products, arithmetic and copies ran while one was open for 25% -> 33% of each run, Pallas kernels for 0% -> 0%
where the time goes in v1:
time: 802 us; the launch traced here: 791 us
  blocking collectives  323 us (40%)
  other arithmetic  311 us (39%)
  matrix products  66.3 us (8%)
  local copies, waits for them, and re-layouts  57.1 us (7%)
  between operations  31.4 us (4%)
    psum x4, blocking collectives, body(): lax.psum((slotted, part_means, own_values, own_errors), ('space', 'member...  323 us
    another operation x28, other arithmetic, innovation(): factor = jnp.linalg.cholesky(innov_cov)  139 us
    another operation x9, other arithmetic, innovation(): lax.linalg.triangular_solve(factor, inverse_sum, left_side=True, lower=Tr...  79.1 us
    another operation x4, other arithmetic, innovation(): lax.linalg.triangular_solve(factor + jnp.diag(errors_now), identity, left...  78.6 us
    another operation x49, local copies, waits for them, and re-layouts, innovation(): lax.linalg.triangular_solve(factor, inverse_sum, left_side=True, lower=Tr...  16.8 us
    another operation x40, local copies, waits for them, and re-layouts, innovation(): lax.linalg.triangular_solve(factor + jnp.diag(errors_now), identity, left...  16.5 us
  transfers between devices with their start and end apart: 4, of which 0 were waited for; matrix products, arithmetic and copies ran while one was open for 33% of the time, Pallas kernels for 0%

profile of v1, /device:TPU:1, one launch (start us, length us, event | category | flops | bytes accessed | tf_op | source)
XLA Modules:
  0.0 790.7 jit_solution(12761173401598143773)
XLA Ops:
  29.0 85.5 %all-reduce.9 = (bf16[4,256,128]{2,1,0:T(8,128)(2,1)S(1)}, f32[256]{0:T(256)S(1)}, f32[256]{0:T(256)S(1)}, f32[256]{0:T(256)S(1)}) all-reduce(f32[4,256,128]{2,1,0:T(8,128)S(1)} %fusion.19, f32[256]{0:T(256)S(1)} %bitcast.641, f32[256]{0:T(256)S(1)} %bitcast.640, ...), channel_id=1, replica_groups=mesh['space'=32,'member'=4,'lag'=2] {'space','member','lag'}, use_global_device_ids=true, to_apply=%region_0.1 | all-reduce | flops 131840 | bytes 792576 | tf_op jit(solution)/shard_map/psum | solution.py:79
  115.0 11.7 %cholesky.214 = f32[128,128]{1,0:T(8,128)S(1)} custom-call(f32[128,128]{1,0:T(8,128)S(1)} %cholesky.346), custom_call_target="Cholesky" | custom-call | tf_op jit(solution)/shard_map/jit(cholesky)/cholesky | solution.py:17
  126.8 9.8 %custom-call.35 = f32[1,128,128]{1,2,0:T(8,128)S(1)} custom-call(f32[1,128,128]{2,1,0:T(8,128)S(1)} %get-tuple-element.366), custom_call_target="InvertDiagBlocksLowerTriangular" | custom-call | tf_op jit(solution)/shard_map/jit(cholesky)/cholesky | solution.py:17
  137.0 11.7 %cholesky.231 = f32[128,128]{1,0:T(8,128)S(1)} custom-call(f32[128,128]{1,0:T(8,128)S(1)} %convolution_subtract_fusion.15), custom_call_target="Cholesky" | custom-call | tf_op jit(solution)/shard_map/jit(cholesky)/cholesky | solution.py:17
  151.8 4.2 while.33
  157.7 4.4 while.32
  164.4 19.7 %custom-call.37 = f32[2,128,128]{1,2,0:T(8,128)S(1)} custom-call(f32[2,128,128]{2,1,0:T(8,128)S(1)} %get-tuple-element.112), custom_call_target="InvertDiagBlocksLowerTriangular" | custom-call | tf_op jit(solution)/shard_map/triangular_solve/custom-call.4 | solution.py:22
  185.0 19.7 %custom-call.36 = f32[2,128,128]{1,2,0:T(8,128)S(1)} custom-call(f32[2,128,128]{2,1,0:T(8,128)S(1)} %get-tuple-element.111), custom_call_target="InvertDiagBlocksLowerTriangular" | custom-call | tf_op jit(solution)/shard_map/triangular_solve/custom-call.0 | solution.py:19
  228.1 79.6 %all-reduce.10 = (bf16[4,256,128]{2,1,0:T(8,128)(2,1)S(1)}, f32[256]{0:T(256)S(1)}, f32[256]{0:T(256)S(1)}, f32[256]{0:T(256)S(1)}) all-reduce(f32[4,256,128]{2,1,0:T(8,128)S(1)} %fusion.18, f32[256]{0:T(256)S(1)} %bitcast.639, f32[256]{0:T(256)S(1)} %bitcast.638, ...), channel_id=1, replica_groups=mesh['space'=32,'member'=4,'lag'=2] {'space','member','lag'}, use_global_device_ids=true, to_apply=%region_7.11 | all-reduce | flops 131840 | bytes 792576 | tf_op jit(solution)/shard_map/psum | solution.py:79
  308.2 11.7 %cholesky.248 = f32[128,128]{1,0:T(8,128)S(1)} custom-call(f32[128,128]{1,0:T(8,128)S(1)} %cholesky.349), custom_call_target="Cholesky" | custom-call | tf_op jit(solution)/shard_map/jit(cholesky)/cholesky | solution.py:17
  320.0 9.8 %custom-call.38 = f32[1,128,128]{1,2,0:T(8,128)S(1)} custom-call(f32[1,128,128]{2,1,0:T(8,128)S(1)} %get-tuple-element.364), custom_call_target="InvertDiagBlocksLowerTriangular" | custom-call | tf_op jit(solution)/shard_map/jit(cholesky)/cholesky | solution.py:17
  330.3 11.7 %cholesky.265 = f32[128,128]{1,0:T(8,128)S(1)} custom-call(f32[128,128]{1,0:T(8,128)S(1)} %convolution_subtract_fusion.14), custom_call_target="Cholesky" | custom-call | tf_op jit(solution)/shard_map/jit(cholesky)/cholesky | solution.py:17
  345.1 4.4 while.35
  349.6 4.2 while.34
  353.8 19.7 %custom-call.40 = f32[2,128,128]{1,2,0:T(8,128)S(1)} custom-call(f32[2,128,128]{2,1,0:T(8,128)S(1)} %get-tuple-element.114), custom_call_target="InvertDiagBlocksLowerTriangular" | custom-call | tf_op jit(solution)/shard_map/triangular_solve/custom-call.4 | solution.py:22
  374.3 19.7 %custom-call.39 = f32[2,128,128]{1,2,0:T(8,128)S(1)} custom-call(f32[2,128,128]{2,1,0:T(8,128)S(1)} %get-tuple-element.113), custom_call_target="InvertDiagBlocksLowerTriangular" | custom-call | tf_op jit(solution)/shard_map/triangular_solve/custom-call.0 | solution.py:19
  416.1 78.8 %all-reduce.11 = (bf16[4,256,128]{2,1,0:T(8,128)(2,1)S(1)}, f32[256]{0:T(256)S(1)}, f32[256]{0:T(256)S(1)}, f32[256]{0:T(256)S(1)}) all-reduce(f32[4,256,128]{2,1,0:T(8,128)S(1)} %fusion.17, f32[256]{0:T(256)S(1)} %bitcast.637, f32[256]{0:T(256)S(1)} %bitcast.636, ...), channel_id=1, replica_groups=mesh['space'=32,'member'=4,'lag'=2] {'space','member','lag'}, use_global_device_ids=true, to_apply=%region_10.14 | all-reduce | flops 131840 | bytes 792576 | tf_op jit(solution)/shard_map/psum | solution.py:79
  495.4 11.7 %cholesky.282 = f32[128,128]{1,0:T(8,128)S(1)} custom-call(f32[128,128]{1,0:T(8,128)S(1)} %cholesky.352), custom_call_target="Cholesky" | custom-call | tf_op jit(solution)/shard_map/jit(cholesky)/cholesky | solution.py:17
  507.1 9.8 %custom-call.41 = f32[1,128,128]{1,2,0:T(8,128)S(1)} custom-call(f32[1,128,128]{2,1,0:T(8,128)S(1)} %get-tuple-element.362), custom_call_target="InvertDiagBlocksLowerTriangular" | custom-call | tf_op jit(solution)/shard_map/jit(cholesky)/cholesky | solution.py:17
  517.4 11.7 %cholesky.299 = f32[128,128]{1,0:T(8,128)S(1)} custom-call(f32[128,128]{1,0:T(8,128)S(1)} %convolution_subtract_fusion.13), custom_call_target="Cholesky" | custom-call | tf_op jit(solution)/shard_map/jit(cholesky)/cholesky | solution.py:17
  532.2 4.4 while.37
  536.6 4.2 while.36
  540.8 19.7 %custom-call.43 = f32[2,128,128]{1,2,0:T(8,128)S(1)} custom-call(f32[2,128,128]{2,1,0:T(8,128)S(1)} %get-tuple-element.116), custom_call_target="InvertDiagBlocksLowerTriangular" | custom-call | tf_op jit(solution)/shard_map/triangular_solve/custom-call.4 | solution.py:22
  561.4 19.7 %custom-call.42 = f32[2,128,128]{1,2,0:T(8,128)S(1)} custom-call(f32[2,128,128]{2,1,0:T(8,128)S(1)} %get-tuple-element.115), custom_call_target="InvertDiagBlocksLowerTriangular" | custom-call | tf_op jit(solution)/shard_map/triangular_solve/custom-call.0 | solution.py:19
  603.2 79.2 %all-reduce.12 = (bf16[4,256,128]{2,1,0:T(8,128)(2,1)S(1)}, f32[256]{0:T(256)S(1)}, f32[256]{0:T(256)S(1)}, f32[256]{0:T(256)S(1)}) all-reduce(f32[4,256,128]{2,1,0:T(8,128)S(1)} %fusion.16, f32[256]{0:T(256)S(1)} %bitcast.635, f32[256]{0:T(256)S(1)} %bitcast.634, ...), channel_id=1, replica_groups=mesh['space'=32,'member'=4,'lag'=2] {'space','member','lag'}, use_global_device_ids=true, to_apply=%region_13.17 | all-reduce | flops 131840 | bytes 792576 | tf_op jit(solution)/shard_map/psum | solution.py:79
  683.0 11.7 %cholesky.316 = f32[128,128]{1,0:T(8,128)S(1)} custom-call(f32[128,128]{1,0:T(8,128)S(1)} %cholesky.355), custom_call_target="Cholesky" | custom-call | tf_op jit(solution)/shard_map/jit(cholesky)/cholesky | solution.py:17
  694.7 9.8 %custom-call.44 = f32[1,128,128]{1,2,0:T(8,128)S(1)} custom-call(f32[1,128,128]{2,1,0:T(8,128)S(1)} %get-tuple-element.360), custom_call_target="InvertDiagBlocksLowerTriangular" | custom-call | tf_op jit(solution)/shard_map/jit(cholesky)/cholesky | solution.py:17
  705.0 11.7 %cholesky.333 = f32[128,128]{1,0:T(8,128)S(1)} custom-call(f32[128,128]{1,0:T(8,128)S(1)} %convolution_subtract_fusion.12), custom_call_target="Cholesky" | custom-call | tf_op jit(solution)/shard_map/jit(cholesky)/cholesky | solution.py:17
  719.9 4.4 while.39
  724.4 4.4 while.38
  728.8 19.9 %custom-call.46 = f32[2,128,128]{1,2,0:T(8,128)S(1)} custom-call(f32[2,128,128]{2,1,0:T(8,128)S(1)} %get-tuple-element.118), custom_call_target="InvertDiagBlocksLowerTriangular" | custom-call | tf_op jit(solution)/shard_map/triangular_solve/custom-call.4 | solution.py:22
  749.6 19.7 %custom-call.45 = f32[2,128,128]{1,2,0:T(8,128)S(1)} custom-call(f32[2,128,128]{2,1,0:T(8,128)S(1)} %get-tuple-element.117), custom_call_target="InvertDiagBlocksLowerTriangular" | custom-call | tf_op jit(solution)/shard_map/triangular_solve/custom-call.0 | solution.py:19
  (430 shorter events, 144.3 us)
Async XLA Ops:
  7.2 9.8 %copy-start.53 = (s32[4,1,4]{2,1,0:T(1,128)S(1)}, s32[4,1,4]{2,1,0:T(1,128)}, u32[]{:S(2)}) copy-start(s32[4,1,4]{2,1,0:T(1,128)} %param.21) | copy-start | bytes 196
  7.2 14.5 %copy-start.16 = (s32[4,1,1]{0,2,1:T(1,128)S(1)}, s32[4,1,1]{0,2,1:T(1,128)}, u32[]{:S(2)}) copy-start(s32[4,1,1]{0,2,1:T(1,128)} %param.22) | copy-start | bytes 52
  7.2 11.4 %copy-start.15 = (s32[4]{0:T(128)S(1)}, s32[4]{0:T(128)}, u32[]{:S(2)}) copy-start(s32[4]{0:T(128)} %param.25) | copy-start | bytes 52
  7.2 203.3 %all-gather.9.cloned.1.call-start = ((), (), s32[]{:S(2)}) async-start(), calls=%async_computation | async-start | bytes 2621440 | tf_op jit(solution)/shard_map/all_gather | solution.py:86
  13.7 11.7 %copy-start.14 = (f32[1,4096]{1,0:T(1,128)S(1)}, f32[1,4096]{1,0:T(1,128)}, u32[]{:S(2)}) copy-start(f32[1,4096]{1,0:T(1,128)} %param.19) | copy-start | bytes 49156
  17.0 7.9 copy-start.24
  17.0 139.0 %copy-start.22 = (s32[4]{0:T(128)}, s32[4]{0:T(128)S(1)}, u32[]{:S(2)}) copy-start(s32[4]{0:T(128)S(1)} %get-tuple-element.376) | copy-start | bytes 52
  17.0 187.7 %copy-start.20 = (s32[4]{0:T(128)}, s32[4]{0:T(128)S(1)}, u32[]{:S(2)}) copy-start(s32[4]{0:T(128)S(1)} %get-tuple-element.378) | copy-start | bytes 52
  17.0 188.3 %copy-start.18 = (s32[4]{0:T(128)}, s32[4]{0:T(128)S(1)}, u32[]{:S(2)}) copy-start(s32[4]{0:T(128)S(1)} %get-tuple-element.375) | copy-start | bytes 52
  18.5 9.9 %copy-start.51 = (f32[1,4,256]{2,1,0:T(4,128)S(1)}, f32[1,4,256]{2,1,0:T(4,128)}, u32[]{:S(2)}) copy-start(f32[1,4,256]{2,1,0:T(4,128)} %param.23) | copy-start | bytes 12292
  18.5 9.9 %copy-start.52 = (f32[1,4,256]{2,1,0:T(4,128)S(1)}, f32[1,4,256]{2,1,0:T(4,128)}, u32[]{:S(2)}) copy-start(f32[1,4,256]{2,1,0:T(4,128)} %param.24) | copy-start | bytes 12292
  18.5 380.0 %all-gather.11.cloned.1.call-start = ((), (), s32[]{:S(2)}) async-start(), calls=%async_computation.1 | async-start | bytes 2621440 | tf_op jit(solution)/shard_map/all_gather | solution.py:86
  23.0 6.0 copy-start.40
  26.7 87.8 %copy-start.12 = (f32[4,512]{1,0:T(4,128)}, f32[4,512]{1,0:T(4,128)S(1)}, u32[]{:S(2)}) copy-start(f32[4,512]{1,0:T(4,128)S(1)} %gather_fusion.4) | copy-start | bytes 24580
  114.5 69.5 %copy-start.8 = (bf16[4,256,128]{2,1,0:T(8,128)(2,1)}, bf16[4,256,128]{2,1,0:T(8,128)(2,1)S(1)}, u32[]{:S(2)}) copy-start(bf16[4,256,128]{2,1,0:T(8,128)(2,1)S(1)} %get-tuple-element.331) | copy-start | bytes 786436
  218.3 4.9 copy-start.41
  226.1 82.0 %copy-start.6 = (bf16[4,512,128]{2,1,0:T(8,128)(2,1)}, bf16[4,512,128]{2,1,0:T(8,128)(2,1)S(1)}, u32[]{:S(2)}) copy-start(bf16[4,512,128]{2,1,0:T(8,128)(2,1)S(1)} %gather_fusion.1) | copy-start | bytes 1572868
  307.7 65.8 %copy-start.10 = (bf16[4,256,128]{2,1,0:T(8,128)(2,1)}, bf16[4,256,128]{2,1,0:T(8,128)(2,1)S(1)}, u32[]{:S(2)}) copy-start(bf16[4,256,128]{2,1,0:T(8,128)(2,1)S(1)} %get-tuple-element.327) | copy-start | bytes 786436
  308.1 37.0 %copy-start.59 = (s32[2,2]{1,0:T(2,128)S(1)}, s32[2,2]{1,0:T(2,128)}, u32[]{:S(2)}) copy-start(s32[2,2]{1,0:T(2,128)} %copy-done.58) | copy-start | bytes 52
  342.3 243.3 %all-gather.13.cloned.1.call-start = ((), (), s32[]{:S(2)}) async-start(), calls=%async_computation.2 | async-start | bytes 2621440 | tf_op jit(solution)/shard_map/all_gather | solution.py:86
  353.8 44.7 %copy-start.60 = (s32[2,2]{1,0:T(2,128)}, s32[2,2]{1,0:T(2,128)S(1)}, u32[]{:S(2)}) copy-start(s32[2,2]{1,0:T(2,128)S(1)} %get-tuple-element.774) | copy-start | bytes 52
  406.3 4.9 copy-start.39
  414.1 81.2 %copy-start.2 = (bf16[4,512,128]{2,1,0:T(8,128)(2,1)}, bf16[4,512,128]{2,1,0:T(8,128)(2,1)S(1)}, u32[]{:S(2)}) copy-start(bf16[4,512,128]{2,1,0:T(8,128)(2,1)S(1)} %gather_fusion.2) | copy-start | bytes 1572868
  494.9 65.6 %copy-start.9 = (bf16[4,256,128]{2,1,0:T(8,128)(2,1)}, bf16[4,256,128]{2,1,0:T(8,128)(2,1)S(1)}, u32[]{:S(2)}) copy-start(bf16[4,256,128]{2,1,0:T(8,128)(2,1)S(1)} %get-tuple-element.323) | copy-start | bytes 786436
  495.3 36.9 %copy-start.61 = (s32[2,2]{1,0:T(2,128)S(1)}, s32[2,2]{1,0:T(2,128)}, u32[]{:S(2)}) copy-start(s32[2,2]{1,0:T(2,128)} %copy-done.60) | copy-start | bytes 52
  529.5 243.8 %all-gather.15.cloned.1.call-start = ((), (), s32[]{:S(2)}) async-start(), calls=%async_computation.3 | async-start | bytes 2621440 | tf_op jit(solution)/shard_map/all_gather | solution.py:86
  540.8 44.8 %copy-start.62 = (s32[2,2]{1,0:T(2,128)}, s32[2,2]{1,0:T(2,128)S(1)}, u32[]{:S(2)}) copy-start(s32[2,2]{1,0:T(2,128)S(1)} %get-tuple-element.776) | copy-start | bytes 52
  593.4 4.9 copy-start.3
  593.4 4.9 copy-start.37
  601.2 81.6 %copy-start.4 = (bf16[4,512,128]{2,1,0:T(8,128)(2,1)}, bf16[4,512,128]{2,1,0:T(8,128)(2,1)S(1)}, u32[]{:S(2)}) copy-start(bf16[4,512,128]{2,1,0:T(8,128)(2,1)S(1)} %gather_fusion.3) | copy-start | bytes 1572868
  682.5 66.3 %copy-start.11 = (bf16[4,256,128]{2,1,0:T(8,128)(2,1)}, bf16[4,256,128]{2,1,0:T(8,128)(2,1)S(1)}, u32[]{:S(2)}) copy-start(bf16[4,256,128]{2,1,0:T(8,128)(2,1)S(1)} %get-tuple-element.319) | copy-start | bytes 786436
  682.9 37.0 %copy-start.63 = (s32[2,2]{1,0:T(2,128)S(1)}, s32[2,2]{1,0:T(2,128)}, u32[]{:S(2)}) copy-start(s32[2,2]{1,0:T(2,128)} %copy-done.62) | copy-start | bytes 52
  (36 other events, 77.0 us)
Sparse Core Ops, SparseCore 0:
  18.6 40.2 all-gather.8
  342.5 32.4 all-gather.10
  529.6 32.3 all-gather.12
  717.2 32.3 all-gather.14

commit v2 on v1

--- a/solution.py
+++ b/solution.py
@@ -10,24 +10,40 @@
 
 
 def innovation(obs_round, values_now, obs_means, errors_now, members):
+    highest = lax.Precision.HIGHEST
     obs_total = obs_round.shape[0]
+    half = obs_total // 2
     innov_cov = jnp.dot(obs_round, obs_round.T, preferred_element_type=jnp.float32) / (
         members - 1
     ) + jnp.diag(errors_now * errors_now)
-    factor = jnp.linalg.cholesky(innov_cov)
-    identity = jnp.eye(obs_total, dtype=jnp.float32)
-    inverse_sum = lax.linalg.triangular_solve(
-        factor + jnp.diag(errors_now), identity, left_side=True, lower=True
+    innov_cov = (innov_cov + innov_cov.T) * 0.5
+    eye = jnp.eye(half, dtype=jnp.float32)
+    eyes = jnp.stack([eye, eye])
+    errors_top, errors_low = errors_now[:half], errors_now[half:]
+    factor_11 = lax.linalg.cholesky(innov_cov[:half, :half], symmetrize_input=False)
+    inv_top = lax.linalg.triangular_solve(
+        jnp.stack([factor_11, factor_11 + jnp.diag(errors_top)]), eyes, left_side=True, lower=True
     )
-    transform = lax.linalg.triangular_solve(
-        factor, inverse_sum, left_side=True, lower=True, transpose_a=True
+    factor_11_inv, sum_11_inv = inv_top[0], inv_top[1]
+    factor_21 = jnp.dot(innov_cov[half:, :half], factor_11_inv.T, precision=highest)
+    schur = innov_cov[half:, half:] - jnp.dot(factor_21, factor_21.T, precision=highest)
+    factor_22 = lax.linalg.cholesky(schur, symmetrize_input=True)
+    inv_low = lax.linalg.triangular_solve(
+        jnp.stack([factor_22, factor_22 + jnp.diag(errors_low)]), eyes, left_side=True, lower=True
     )
-    forward = lax.linalg.triangular_solve(
-        factor, (values_now - obs_means)[:, None], left_side=True, lower=True
+    factor_22_inv, sum_22_inv = inv_low[0], inv_low[1]
+    factor_21_inv = -jnp.dot(
+        factor_22_inv, jnp.dot(factor_21, factor_11_inv, precision=highest), precision=highest
     )
-    weights_obs = lax.linalg.triangular_solve(
-        factor, forward, left_side=True, lower=True, transpose_a=True
-    )[:, 0]
+    sum_21_inv = -jnp.dot(
+        sum_22_inv, jnp.dot(factor_21, sum_11_inv, precision=highest), precision=highest
+    )
+    zeros = jnp.zeros((half, half), jnp.float32)
+    factor_inv = jnp.block([[factor_11_inv, zeros], [factor_21_inv, factor_22_inv]])
+    inverse_sum = jnp.block([[sum_11_inv, zeros], [sum_21_inv, sum_22_inv]])
+    transform = jnp.dot(factor_inv.T, inverse_sum, precision=highest)
+    forward = jnp.dot(factor_inv, values_now - obs_means, precision=highest)
+    weights_obs = jnp.dot(factor_inv.T, forward, precision=highest)
     return (transform, weights_obs)
 
 

time: 802 us -> 723 us (0.901)
  other arithmetic: 311 us -> 273 us
  local copies, waits for them, and re-layouts: 57.1 us -> 28.3 us
    another operation x121 -> x4, local copies, waits for them, and re-layouts: 34.7 us -> 0.14 us  [the longest x49 16.8 us: innovation(): lax.linalg.triangular_solve(factor, inverse_sum, left_side=True, lower=Tr...]
    another operation x41 -> x49, other arithmetic: 296 us -> 264 us  [the longest x9 79.9 us: innovation(): lax.linalg.triangular_solve(jnp.stack([factor_11, factor_11 + jnp.diag(er...]
    another operation x56 -> x8, matrix products: 17.8 us -> 3.09 us  [the longest x4 1.54 us: innovation(): lax.linalg.triangular_solve(jnp.stack([factor_11, factor_11 + jnp.diag(er...]
    dot_general x0 -> x36, matrix products: none -> 14.2 us  [the longest x4 4.81 us: innovation(): transform = jnp.dot(factor_inv.T, inverse_sum, precision=highest)]
  transfers between devices with their start and end apart: 4 -> 4, of which waited for: 0 -> 0; matrix products, arithmetic and copies ran while one was open for 33% -> 45% of each run, Pallas kernels for 0% -> 0%
where the time goes in v2:
time: 723 us; the launch traced here: 715 us
  blocking collectives  327 us (45%)
  other arithmetic  273 us (38%)
  matrix products  61.1 us (8%)
  local copies, waits for them, and re-layouts  28.3 us (4%)
  between operations  25.7 us (4%)
    psum x4, blocking collectives, body(): lax.psum((slotted, part_means, own_values, own_errors), ('space', 'member...  327 us
    another operation x9, other arithmetic, innovation(): lax.linalg.triangular_solve(jnp.stack([factor_11, factor_11 + jnp.diag(er...  79.9 us
    another operation x8, other arithmetic, innovation(): lax.linalg.triangular_solve(jnp.stack([factor_22, factor_22 + jnp.diag(er...  78.8 us
    another operation x12, other arithmetic, innovation(): lax.linalg.cholesky(innov_cov[:half, :half], symmetrize_input=False)  49.6 us
    another operation x12, other arithmetic, innovation(): factor_22 = lax.linalg.cholesky(schur, symmetrize_input=True)  49.6 us
  transfers between devices with their start and end apart: 4, of which 0 were waited for; matrix products, arithmetic and copies ran while one was open for 45% of the time, Pallas kernels for 0%

profile of v2, /device:TPU:1, one launch (start us, length us, event | category | flops | bytes accessed | tf_op | source)
XLA Modules:
  0.0 715.1 jit_solution(16916640992161307852)
XLA Ops:
  19.8 1.9 fusion.15
  28.9 85.5 %all-reduce.16 = (bf16[4,256,128]{2,1,0:T(8,128)(2,1)S(1)}, f32[256]{0:T(256)S(1)}, f32[256]{0:T(256)S(1)}, f32[256]{0:T(256)S(1)}) all-reduce(f32[4,256,128]{2,1,0:T(8,128)S(1)} %fusion.15, f32[256]{0:T(256)S(1)} %bitcast.471, f32[256]{0:T(256)S(1)} %bitcast.470, ...), channel_id=1, replica_groups=mesh['space'=32,'member'=4,'lag'=2] {'space','member','lag'}, use_global_device_ids=true, to_apply=%region_0.1 | all-reduce | flops 131840 | bytes 792576 | tf_op jit(solution)/shard_map/psum | solution.py:95
  115.0 11.7 %custom-call.20 = f32[128,128]{1,0:T(8,128)S(1)} custom-call(f32[128,128]{1,0:T(8,128)S(1)} %slice.180), custom_call_target="Cholesky" | custom-call | tf_op jit(solution)/shard_map/cholesky/custom-call.1 | solution.py:23
  128.0 20.1 %custom-call.21 = f32[2,1,128,128]{2,3,1,0:T(8,128)S(1)} custom-call(f32[2,1,128,128]{3,2,1,0:T(8,128)S(1)} %fusion.95), custom_call_target="InvertDiagBlocksLowerTriangular" | custom-call | tf_op jit(solution)/shard_map/triangular_solve/custom-call.0 | solution.py:24
  149.2 11.7 %custom-call.22 = f32[128,128]{1,0:T(8,128)S(1)} custom-call(f32[128,128]{1,0:T(8,128)S(1)} %fusion.125), custom_call_target="Cholesky" | custom-call | tf_op jit(solution)/shard_map/cholesky/custom-call.1 | solution.py:30
  163.3 19.7 %custom-call.23 = f32[2,1,128,128]{2,3,1,0:T(8,128)S(1)} custom-call(f32[2,1,128,128]{3,2,1,0:T(8,128)S(1)} %fusion.96), custom_call_target="InvertDiagBlocksLowerTriangular" | custom-call | tf_op jit(solution)/shard_map/triangular_solve/custom-call.0 | solution.py:31
  191.1 2.4 fusion.261
  196.5 2.1 scatter_fusion
  202.9 1.9 fusion.265
  207.8 80.7 %all-reduce.17 = (bf16[4,256,128]{2,1,0:T(8,128)(2,1)S(1)}, f32[256]{0:T(256)S(1)}, f32[256]{0:T(256)S(1)}, f32[256]{0:T(256)S(1)}) all-reduce(f32[4,256,128]{2,1,0:T(8,128)} %copy-done.6, f32[256]{0:T(256)} %bitcast.469, f32[256]{0:T(256)} %bitcast.468, ...), channel_id=1, replica_groups=mesh['space'=32,'member'=4,'lag'=2] {'space','member','lag'}, use_global_device_ids=true, to_apply=%region_5.8 | all-reduce | flops 131840 | bytes 792576 | tf_op jit(solution)/shard_map/psum | solution.py:95
  289.0 11.7 %custom-call.24 = f32[128,128]{1,0:T(8,128)S(1)} custom-call(f32[128,128]{1,0:T(8,128)S(1)} %slice.187), custom_call_target="Cholesky" | custom-call | tf_op jit(solution)/shard_map/cholesky/custom-call.1 | solution.py:23
  302.1 19.9 %custom-call.25 = f32[2,1,128,128]{2,3,1,0:T(8,128)S(1)} custom-call(f32[2,1,128,128]{3,2,1,0:T(8,128)S(1)} %fusion.97), custom_call_target="InvertDiagBlocksLowerTriangular" | custom-call | tf_op jit(solution)/shard_map/triangular_solve/custom-call.0 | solution.py:24
  323.9 11.7 %custom-call.26 = f32[128,128]{1,0:T(8,128)S(1)} custom-call(f32[128,128]{1,0:T(8,128)S(1)} %fusion.123), custom_call_target="Cholesky" | custom-call | tf_op jit(solution)/shard_map/cholesky/custom-call.1 | solution.py:30
  337.0 19.7 %custom-call.27 = f32[2,1,128,128]{2,3,1,0:T(8,128)S(1)} custom-call(f32[2,1,128,128]{3,2,1,0:T(8,128)S(1)} %fusion.98), custom_call_target="InvertDiagBlocksLowerTriangular" | custom-call | tf_op jit(solution)/shard_map/triangular_solve/custom-call.0 | solution.py:31
  360.3 2.3 fusion.262
  369.4 1.9 fusion.13
  372.1 1.9 fusion.266
  376.9 80.0 %all-reduce.18 = (bf16[4,256,128]{2,1,0:T(8,128)(2,1)S(1)}, f32[256]{0:T(256)S(1)}, f32[256]{0:T(256)S(1)}, f32[256]{0:T(256)S(1)}) all-reduce(f32[4,256,128]{2,1,0:T(8,128)} %copy-done.7, f32[256]{0:T(256)} %bitcast.467, f32[256]{0:T(256)} %bitcast.466, ...), channel_id=1, replica_groups=mesh['space'=32,'member'=4,'lag'=2] {'space','member','lag'}, use_global_device_ids=true, to_apply=%region_8.11 | all-reduce | flops 131840 | bytes 792576 | tf_op jit(solution)/shard_map/psum | solution.py:95
  457.7 11.7 %custom-call.28 = f32[128,128]{1,0:T(8,128)S(1)} custom-call(f32[128,128]{1,0:T(8,128)S(1)} %copy.109), custom_call_target="Cholesky" | custom-call | tf_op jit(solution)/shard_map/cholesky/custom-call.1 | solution.py:23
  471.0 19.8 %custom-call.29 = f32[2,1,128,128]{2,3,1,0:T(8,128)S(1)} custom-call(f32[2,1,128,128]{3,2,1,0:T(8,128)S(1)} %fusion.99), custom_call_target="InvertDiagBlocksLowerTriangular" | custom-call | tf_op jit(solution)/shard_map/triangular_solve/custom-call.0 | solution.py:24
  492.8 11.7 %custom-call.30 = f32[128,128]{1,0:T(8,128)S(1)} custom-call(f32[128,128]{1,0:T(8,128)S(1)} %fusion.121), custom_call_target="Cholesky" | custom-call | tf_op jit(solution)/shard_map/cholesky/custom-call.1 | solution.py:30
  506.1 19.7 %custom-call.31 = f32[2,1,128,128]{2,3,1,0:T(8,128)S(1)} custom-call(f32[2,1,128,128]{3,2,1,0:T(8,128)S(1)} %fusion.100), custom_call_target="InvertDiagBlocksLowerTriangular" | custom-call | tf_op jit(solution)/shard_map/triangular_solve/custom-call.0 | solution.py:31
  529.4 2.3 fusion.263
  534.8 1.9 scatter_fusion.2
  540.9 1.9 fusion.267
  545.7 80.5 %all-reduce.19 = (bf16[4,256,128]{2,1,0:T(8,128)(2,1)S(1)}, f32[256]{0:T(256)S(1)}, f32[256]{0:T(256)S(1)}, f32[256]{0:T(256)S(1)}) all-reduce(f32[4,256,128]{2,1,0:T(8,128)} %copy-done.5, f32[256]{0:T(256)} %bitcast.465, f32[256]{0:T(256)S(1)} %bitcast.464, ...), channel_id=1, replica_groups=mesh['space'=32,'member'=4,'lag'=2] {'space','member','lag'}, use_global_device_ids=true, to_apply=%region_11.14 | all-reduce | flops 131840 | bytes 792576 | tf_op jit(solution)/shard_map/psum | solution.py:95
  626.8 11.7 %custom-call.32 = f32[128,128]{1,0:T(8,128)S(1)} custom-call(f32[128,128]{1,0:T(8,128)S(1)} %copy.126), custom_call_target="Cholesky" | custom-call | tf_op jit(solution)/shard_map/cholesky/custom-call.1 | solution.py:23
  640.0 19.9 %custom-call.33 = f32[2,1,128,128]{2,3,1,0:T(8,128)S(1)} custom-call(f32[2,1,128,128]{3,2,1,0:T(8,128)S(1)} %fusion.101), custom_call_target="InvertDiagBlocksLowerTriangular" | custom-call | tf_op jit(solution)/shard_map/triangular_solve/custom-call.0 | solution.py:24
  662.0 11.7 %custom-call.34 = f32[128,128]{1,0:T(8,128)S(1)} custom-call(f32[128,128]{1,0:T(8,128)S(1)} %broadcast_multiply_fusion.1), custom_call_target="Cholesky" | custom-call | tf_op jit(solution)/shard_map/cholesky/custom-call.1 | solution.py:30
  675.1 19.7 %custom-call.35 = f32[2,1,128,128]{2,3,1,0:T(8,128)S(1)} custom-call(f32[2,1,128,128]{3,2,1,0:T(8,128)S(1)} %fusion.102), custom_call_target="InvertDiagBlocksLowerTriangular" | custom-call | tf_op jit(solution)/shard_map/triangular_solve/custom-call.0 | solution.py:31
  697.9 2.3 fusion.264
  705.0 1.9 fusion.268
  (273 shorter events, 86.0 us)
Async XLA Ops:
  7.2 9.6 %copy-start.29 = (s32[4,1,4]{2,1,0:T(1,128)S(1)}, s32[4,1,4]{2,1,0:T(1,128)}, u32[]{:S(2)}) copy-start(s32[4,1,4]{2,1,0:T(1,128)} %param.15) | copy-start | bytes 196
  7.2 11.2 %copy-start.14 = (s32[4,1,1]{0,2,1:T(1,128)S(1)}, s32[4,1,1]{0,2,1:T(1,128)}, u32[]{:S(2)}) copy-start(s32[4,1,1]{0,2,1:T(1,128)} %param.16) | copy-start | bytes 52
  7.2 183.9 %all-gather.9.cloned.1.call-start = ((), (), s32[]{:S(2)}) async-start(), calls=%async_computation | async-start | bytes 2621440 | tf_op jit(solution)/shard_map/all_gather | solution.py:102
  8.5 13.2 %copy-start.15 = (s32[4]{0:T(128)S(1)}, s32[4]{0:T(128)}, u32[]{:S(2)}) copy-start(s32[4]{0:T(128)} %param.19) | copy-start | bytes 52
  13.7 11.6 %copy-start.13 = (f32[1,4096]{1,0:T(1,128)S(1)}, f32[1,4096]{1,0:T(1,128)}, u32[]{:S(2)}) copy-start(f32[1,4096]{1,0:T(1,128)} %param.13) | copy-start | bytes 49156
  16.8 7.9 %copy-start.17 = (s32[4]{0:T(128)}, s32[4]{0:T(128)S(1)}, u32[]{:S(2)}) copy-start(s32[4]{0:T(128)S(1)} %get-tuple-element.62) | copy-start | bytes 52
  18.3 9.9 %copy-start.27 = (f32[1,4,256]{2,1,0:T(4,128)S(1)}, f32[1,4,256]{2,1,0:T(4,128)}, u32[]{:S(2)}) copy-start(f32[1,4,256]{2,1,0:T(4,128)} %param.17) | copy-start | bytes 12292
  18.3 10.0 %copy-start.28 = (f32[1,4,256]{2,1,0:T(4,128)S(1)}, f32[1,4,256]{2,1,0:T(4,128)}, u32[]{:S(2)}) copy-start(f32[1,4,256]{2,1,0:T(4,128)} %param.18) | copy-start | bytes 12292
  18.3 342.0 %all-gather.11.cloned.1.call-start = ((), (), s32[]{:S(2)}) async-start(), calls=%async_computation.1 | async-start | bytes 2621440 | tf_op jit(solution)/shard_map/all_gather | solution.py:102
  19.7 94.7 %copy-start.20 = (pred[4]{0:T(512)(128)(4,1)}, pred[4]{0:T(512)(128)(4,1)S(1)}, u32[]{:S(2)}) copy-start(pred[4]{0:T(512)(128)(4,1)S(1)} %iota_compare_fusion.13) | copy-start | bytes 16
  191.1 2.4 copy-start.9
  193.5 1.8 copy-start.1
  193.5 1.8 copy-start.21
  196.5 3.7 copy-start.23
  198.7 4.2 copy-start.30
  200.1 329.3 %all-gather.13.cloned.1.call-start = ((), (), s32[]{:S(2)}) async-start(), calls=%async_computation.2 | async-start | bytes 2621440 | tf_op jit(solution)/shard_map/all_gather | solution.py:102
  200.2 4.5 copy-start.22
  360.3 2.4 copy-start.10
  362.7 1.8 copy-start.4
  362.7 1.8 copy-start.24
  365.8 3.6 copy-start.19
  367.5 4.6 copy-start.31
  368.9 328.9 %all-gather.15.cloned.1.call-start = ((), (), s32[]{:S(2)}) async-start(), calls=%async_computation.3 | async-start | bytes 2621440 | tf_op jit(solution)/shard_map/all_gather | solution.py:102
  369.4 4.5 copy-start.25
  529.4 2.3 copy-start.11
  531.7 1.8 copy-start.3
  534.8 3.4 copy-start.18
  536.7 4.2 copy-start.32
  540.9 4.8 copy-start.26
  542.7 83.9 %copy-start.8 = (pred[256,256]{0,1:T(8,128)(4,1)S(1)}, pred[256,256]{0,1:T(8,128)(4,1)}, u32[]{:S(2)}) copy-start(pred[256,256]{0,1:T(8,128)(4,1)} %copy.123) | copy-start | bytes 196612
  697.8 2.4 copy-start.12
  705.0 3.2 copy-start
  (5 other events, 5.5 us)
Sparse Core Ops, SparseCore 0:
  18.4 40.1 all-gather.8
  200.2 34.2 all-gather.10
  369.0 33.6 all-gather.12
  538.3 34.1 all-gather.14

commit v3 on v2

--- a/solution.py
+++ b/solution.py
@@ -65,61 +65,86 @@
     member_dev = anomalies.shape[2]
     groups = lax.axis_size("member")
     members = member_dev * groups
-    tile_anoms = anomalies[0].reshape(-1, tile_cells, member_dev)
-    tile_means = mean_state[0].reshape(-1, tile_cells)
     me_member = lax.axis_index("member")
     me_space = lax.axis_index("space")
     me_lag = lax.axis_index("lag")
     lead = (me_member == 0) & (me_lag == 0)
+    tile_anoms = anomalies[0].reshape(-1, tile_cells, member_dev)
+    tile_means = mean_state[0].reshape(-1, tile_cells)
+    tiles_dev = tile_anoms.shape[0]
+    all_tiles = lax.all_gather(tile_anoms, "member", axis=2, tiled=True)
+    local_ids = jnp.arange(tiles_dev, dtype=jnp.int32)
+    slot_place = jnp.arange(slot_dev, dtype=jnp.int32)
+    pattern = jnp.zeros((tiles_dev,), jnp.int32)
+    pieces, mean_parts, value_parts, error_parts = [], [], [], []
     for position in range(batches):
         batch_now = batch_order[position]
+        tile_ids = slot_tiles[batch_now, 0]
+        live_slot = slot_place < slot_counts[batch_now, 0, 0]
+        prints = footprints[batch_now, 0]
+        slot_anoms = tile_anoms[tile_ids]
+        slot_means = tile_means[tile_ids].astype(jnp.float32)
+        proj = jnp.einsum("spt,stm->spm", prints, slot_anoms, preferred_element_type=jnp.float32)
+        n_pat = 2**position
+        select = live_slot[:, None] & (
+            pattern[tile_ids][:, None] == jnp.arange(n_pat, dtype=jnp.int32)[None, :]
+        )
+        pieces.append(jnp.sum(jnp.where(select[:, :, None, None], proj[:, None], 0.0), axis=0))
+        masked_mean = jnp.where(live_slot[:, None], slot_means, 0.0)
+        mean_parts.append(
+            jnp.einsum("spt,st->p", prints.astype(jnp.float32), masked_mean, precision=highest)
+        )
         owner_here = lead & (me_space == owners[batch_now])
-        own_values = jnp.where(owner_here, obs_values[0, batch_now], 0)
-        own_errors = jnp.where(owner_here, obs_errors[0, batch_now], 0)
-        tile_ids = slot_tiles[batch_now, 0]
-        live_count = slot_counts[batch_now, 0, 0]
-        live_mask = jnp.arange(slot_dev) < live_count
-        slot_anoms = tile_anoms[tile_ids]
-        slot_means = tile_means[tile_ids]
-        prints = footprints[batch_now, 0]
-        mean_round = slot_means.astype(jnp.bfloat16)
-        masked = jnp.where(live_mask[:, None, None], slot_anoms, 0)
-        part_anoms = jnp.einsum("spt,stm->pm", prints, masked, preferred_element_type=jnp.float32)
-        masked_mean = jnp.where(live_mask[:, None], mean_round, 0)
-        part_means = jnp.einsum(
-            "spt,st->p", prints, masked_mean, preferred_element_type=jnp.float32
+        value_parts.append(jnp.where(owner_here, obs_values[0, batch_now], 0.0))
+        error_parts.append(jnp.where(owner_here, obs_errors[0, batch_now], 0.0))
+        live_tile = jnp.any((tile_ids[:, None] == local_ids[None, :]) & live_slot[:, None], axis=0)
+        pattern = pattern + jnp.where(live_tile, 1 << position, 0)
+    projected = jnp.concatenate(pieces, axis=0)
+    slotted = jnp.zeros((projected.shape[0], groups) + projected.shape[1:], jnp.float32)
+    slotted = lax.dynamic_update_index_in_dim(slotted, projected, me_member, 1)
+    mean_parts = jnp.where(me_member == 0, jnp.stack(mean_parts), 0.0)
+    summed, obs_means_base, values_all, errors_all = lax.psum(
+        (slotted, mean_parts, jnp.stack(value_parts), jnp.stack(error_parts)),
+        ("space", "member", "lag"),
+    )
+    summed = summed.astype(jnp.bfloat16)
+    summed = jnp.transpose(summed, (0, 2, 1, 3)).reshape(summed.shape[0], summed.shape[2], members)
+    transforms = [jnp.eye(members, dtype=jnp.float32)]
+    shifts = [jnp.zeros((members,), jnp.float32)]
+    offset = 0
+    for position in range(batches):
+        n_pat = 2**position
+        part = summed[offset : offset + n_pat].astype(jnp.float32)
+        offset += n_pat
+        obs_anoms = jnp.einsum("spm,smn->pn", part, jnp.stack(transforms), precision=highest)
+        obs_means = obs_means_base[position] + jnp.einsum(
+            "spm,sm->p", part, jnp.stack(shifts), precision=highest
         )
-        slotted = jnp.zeros((groups,) + part_anoms.shape, jnp.float32)
-        slotted = lax.dynamic_update_index_in_dim(slotted, part_anoms, me_member, 0)
-        part_means = jnp.where(me_member == 0, part_means, 0)
-        all_anoms_obs, obs_means, values_now, errors_now = lax.psum(
-            (slotted, part_means, own_values, own_errors), ("space", "member", "lag")
+        obs_round = obs_anoms.astype(jnp.bfloat16)
+        transform, weights_obs = innovation(
+            obs_round, values_all[position], obs_means, errors_all[position], members
         )
-        all_round = all_anoms_obs.astype(jnp.bfloat16)
-        own_round = lax.dynamic_index_in_dim(all_round, me_member, 0, keepdims=False)
-        obs_round = jnp.transpose(all_round, (1, 0, 2)).reshape(all_round.shape[1], -1)
-        transform, weights_obs = innovation(obs_round, values_now, obs_means, errors_now, members)
-        all_anoms = lax.all_gather(slot_anoms, "member", axis=2, tiled=True)
-        covariance = jnp.einsum(
-            "stm,pm->stp", all_anoms, obs_round, preferred_element_type=jnp.float32
-        )
-        gain_tile = (
-            jnp.einsum("stp,pq->stq", covariance, transform, precision=highest) / (members - 1)
-        ).astype(jnp.bfloat16)
-        shift_mean = jnp.einsum("stp,p->st", covariance, weights_obs, precision=highest) / (
-            members - 1
-        )
-        step_anoms = jnp.einsum(
-            "stp,pm->stm", gain_tile, own_round, preferred_element_type=jnp.float32
-        )
-        updated = (slot_anoms.astype(jnp.float32) - step_anoms).astype(jnp.bfloat16)
-        tile_anoms = tile_anoms.at[tile_ids].set(
-            jnp.where(live_mask[:, None, None], updated, slot_anoms)
-        )
-        tile_means = tile_means.at[tile_ids].set(
-            jnp.where(live_mask[:, None], slot_means + shift_mean, slot_means)
-        )
-    return (tile_anoms.reshape(1, -1, member_dev), tile_means.reshape(1, -1))
+        wide_obs = obs_round.astype(jnp.float32)
+        step = jnp.dot(
+            wide_obs.T, jnp.dot(transform, wide_obs, precision=highest), precision=highest
+        ) / (members - 1)
+        lift = jnp.dot(wide_obs.T, weights_obs, precision=highest) / (members - 1)
+        new_transforms = [t - jnp.dot(t, step, precision=highest) for t in transforms]
+        new_shifts = [s + jnp.dot(t, lift, precision=highest) for t, s in zip(transforms, shifts)]
+        transforms = transforms + new_transforms
+        shifts = shifts + new_shifts
+    own_cols = lax.dynamic_slice_in_dim(
+        jnp.stack(transforms), me_member * member_dev, member_dev, axis=2
+    )
+    tile_transform = own_cols[pattern]
+    tile_shift = jnp.stack(shifts)[pattern]
+    wide_tiles = all_tiles.astype(jnp.float32)
+    updated = jnp.einsum("tcm,tmn->tcn", wide_tiles, tile_transform, precision=highest)
+    touched = pattern > 0
+    new_anoms = jnp.where(touched[:, None, None], updated.astype(jnp.bfloat16), tile_anoms)
+    shift_mean = jnp.einsum("tcm,tm->tc", wide_tiles, tile_shift, precision=highest)
+    new_means = jnp.where(touched[:, None], tile_means + shift_mean, tile_means)
+    return (new_anoms.reshape(1, -1, member_dev), new_means.reshape(1, -1))
 
 
 def solution(mesh):

time: 723 us -> 771 us (1.066)
  blocking collectives: 327 us -> 148 us
  matrix products: 61.1 us -> 152 us
  local copies, waits for them, and re-layouts: 28.3 us -> 119 us
  other arithmetic: 273 us -> 315 us
    psum x4 -> x1, blocking collectives: 327 us -> 148 us  [body(): lax.psum((slotted, mean_parts, jnp.stack(value_parts), jnp.stack(error_pa...]
    dot_general x24 -> x60, matrix products: 42.7 us -> 115 us  [the longest x15 44.5 us: body(): jnp.dot(t, step, precision=highest)]
    dynamic_update_slice x0 -> x1, local copies, waits for them, and re-layouts: none -> 51.6 us  [body(): slotted = lax.dynamic_update_index_in_dim(slotted, projected, me_member, 1)]
    slice x4 -> x9, local copies, waits for them, and re-layouts: 0.02 us -> 14.6 us  [the longest x7 13.4 us: body(): part = summed[offset:offset + n_pat].astype(jnp.float32)]
    add x0 -> x11, other arithmetic: none -> 8.08 us  [body(): s + jnp.dot(t, lift, precision=highest)]
  transfers between devices with their start and end apart: 4 -> 1, of which waited for: 0 -> 0; matrix products, arithmetic and copies ran while one was open for 45% -> 75% of each run, Pallas kernels for 0% -> 0%
where the time goes in v3:
time: 771 us; the launch traced here: 760 us
  other arithmetic  315 us (41%)
  matrix products  152 us (20%)
  blocking collectives  148 us (19%)
  local copies, waits for them, and re-layouts  119 us (15%)
  between operations  25.5 us (3%)
    psum x1, blocking collectives, body(): lax.psum((slotted, mean_parts, jnp.stack(value_parts), jnp.stack(error_pa...  148 us
    another operation x9, other arithmetic, innovation(): lax.linalg.triangular_solve(jnp.stack([factor_11, factor_11 + jnp.diag(er...  84.1 us
    another operation x8, other arithmetic, innovation(): lax.linalg.triangular_solve(jnp.stack([factor_22, factor_22 + jnp.diag(er...  83.5 us
    another operation x12, other arithmetic, innovation(): factor_22 = lax.linalg.cholesky(schur, symmetrize_input=True)  54.2 us
    dynamic_update_slice x1, local copies, waits for them, and re-layouts, body(): slotted = lax.dynamic_update_index_in_dim(slotted, projected, me_member, 1)  51.6 us
    another operation x12, other arithmetic, innovation(): lax.linalg.cholesky(innov_cov[:half, :half], symmetrize_input=False)  51.2 us
    dot_general x15, matrix products, body(): jnp.dot(t, step, precision=highest)  44.5 us
    dot_general x15, matrix products, body(): jnp.dot(t, lift, precision=highest)  18.8 us
  transfers between devices with their start and end apart: 1, of which 0 were waited for; matrix products, arithmetic and copies ran while one was open for 75% of the time, Pallas kernels for 0%

profile of v3, /device:TPU:1, one launch (start us, length us, event | category | flops | bytes accessed | tf_op | source)
XLA Modules:
  0.0 760.2 jit_solution(14129815671907206061)
XLA Ops:
  48.7 4.6 broadcast_in_dim.343
  53.4 51.6 %dynamic_update_slice.4 = f32[15,4,256,128]{3,1,2,0:T(4,128)} dynamic-update-slice(f32[15,4,256,128]{3,1,2,0:T(4,128)} %broadcast_in_dim.343, f32[15,1,256,128]{3,1,2,0:T(1,128)S(1)} %bitcast.626, s32[]{:T(128)} %constant.82.clone.1, s32[]{:T(128)S(6)} %select_n.431, s32[]{:T(128)} %constant.82.clone.1, s32[]{:T(128)} %constant.82.clone.1) | dynamic-update-slice | bytes 3932164 | tf_op jit(solution)/shard_map/jit(dynamic_update_index_in_dim)/dynamic_update_slice | solution.py:104
  117.2 147.8 %all-reduce.11 = (bf16[15,4,256,128]{3,1,2,0:T(4,128)(2,1)}, f32[4,256]{1,0:T(4,128)S(1)}, f32[4,256]{1,0:T(4,128)S(1)}, f32[4,256]{1,0:T(4,128)S(1)}) all-reduce(f32[15,4,256,128]{3,1,2,0:T(4,128)} %dynamic_update_slice.4, ...), channel_id=1, replica_groups=mesh['space'=32,'member'=4,'lag'=2] {'space','member','lag'}, use_global_device_ids=true, to_apply=%region_8.9 | all-reduce | flops 1969152 | bytes 11821056 | tf_op jit(solution)/shard_map/psum | solution.py:106
  267.9 11.7 %custom-call.20 = f32[128,128]{1,0:T(8,128)S(1)} custom-call(f32[128,128]{1,0:T(8,128)S(1)} %slice.287), custom_call_target="Cholesky" | custom-call | tf_op jit(solution)/shard_map/cholesky/custom-call.1 | solution.py:23
  281.0 19.9 %custom-call.21 = f32[2,1,128,128]{2,3,1,0:T(8,128)S(1)} custom-call(f32[2,1,128,128]{3,2,1,0:T(8,128)S(1)} %fusion.134), custom_call_target="InvertDiagBlocksLowerTriangular" | custom-call | tf_op jit(solution)/shard_map/triangular_solve/custom-call.0 | solution.py:24
  306.4 11.7 %custom-call.22 = f32[128,128]{1,0:T(8,128)S(1)} custom-call(f32[128,128]{1,0:T(8,128)S(1)} %fusion.160), custom_call_target="Cholesky" | custom-call | tf_op jit(solution)/shard_map/cholesky/custom-call.1 | solution.py:30
  319.5 20.1 %custom-call.23 = f32[2,1,128,128]{2,3,1,0:T(8,128)S(1)} custom-call(f32[2,1,128,128]{3,2,1,0:T(8,128)S(1)} %fusion.135), custom_call_target="InvertDiagBlocksLowerTriangular" | custom-call | tf_op jit(solution)/shard_map/triangular_solve/custom-call.0 | solution.py:31
  346.5 11.7 %custom-call.24 = f32[128,128]{1,0:T(8,128)S(1)} custom-call(f32[128,128]{1,0:T(8,128)S(1)} %slice.298), custom_call_target="Cholesky" | custom-call | tf_op jit(solution)/shard_map/cholesky/custom-call.1 | solution.py:23
  359.7 19.8 %custom-call.25 = f32[2,1,128,128]{2,3,1,0:T(8,128)S(1)} custom-call(f32[2,1,128,128]{3,2,1,0:T(8,128)S(1)} %fusion.136), custom_call_target="InvertDiagBlocksLowerTriangular" | custom-call | tf_op jit(solution)/shard_map/triangular_solve/custom-call.0 | solution.py:24
  385.3 11.7 %custom-call.26 = f32[128,128]{1,0:T(8,128)S(1)} custom-call(f32[128,128]{1,0:T(8,128)S(1)} %fusion.159), custom_call_target="Cholesky" | custom-call | tf_op jit(solution)/shard_map/cholesky/custom-call.1 | solution.py:30
  399.1 19.7 %custom-call.27 = f32[2,1,128,128]{2,3,1,0:T(8,128)S(1)} custom-call(f32[2,1,128,128]{3,2,1,0:T(8,128)S(1)} %fusion.137), custom_call_target="InvertDiagBlocksLowerTriangular" | custom-call | tf_op jit(solution)/shard_map/triangular_solve/custom-call.0 | solution.py:31
  429.1 3.3 constant_dynamic-update-slice_fusion
  432.4 3.4 fusion.40
  444.6 12.5 %custom-call.28 = f32[128,128]{1,0:T(8,128)S(1)} custom-call(f32[128,128]{1,0:T(8,128)} %copy.169), custom_call_target="Cholesky" | custom-call | tf_op jit(solution)/shard_map/cholesky/custom-call.1 | solution.py:23
  460.1 21.5 %custom-call.29 = f32[2,1,128,128]{2,3,1,0:T(8,128)} custom-call(f32[2,1,128,128]{3,2,1,0:T(8,128)} %fusion.138), custom_call_target="InvertDiagBlocksLowerTriangular" | custom-call | tf_op jit(solution)/shard_map/triangular_solve/custom-call.0 | solution.py:24
  493.2 13.2 %custom-call.30 = f32[128,128]{1,0:T(8,128)} custom-call(f32[128,128]{1,0:T(8,128)} %fusion.158), custom_call_target="Cholesky" | custom-call | tf_op jit(solution)/shard_map/cholesky/custom-call.1 | solution.py:30
  510.1 21.1 %custom-call.31 = f32[2,1,128,128]{2,3,1,0:T(8,128)} custom-call(f32[2,1,128,128]{3,2,1,0:T(8,128)} %fusion.139), custom_call_target="InvertDiagBlocksLowerTriangular" | custom-call | tf_op jit(solution)/shard_map/triangular_solve/custom-call.0 | solution.py:31
  542.5 3.6 slice.318
  548.3 4.3 slice.238
  559.0 3.7 bitcast_dynamic-update-slice_fusion.5
  562.7 3.7 bitcast_dynamic-update-slice_fusion.3
  566.3 3.6 bitcast_dynamic-update-slice_fusion.1
  570.0 6.7 fusion.36
  584.7 12.5 %custom-call.32 = f32[128,128]{1,0:T(8,128)S(1)} custom-call(f32[128,128]{1,0:T(8,128)} %copy.185), custom_call_target="Cholesky" | custom-call | tf_op jit(solution)/shard_map/cholesky/custom-call.1 | solution.py:23
  600.1 21.5 %custom-call.33 = f32[2,1,128,128]{2,3,1,0:T(8,128)} custom-call(f32[2,1,128,128]{3,2,1,0:T(8,128)} %fusion.140), custom_call_target="InvertDiagBlocksLowerTriangular" | custom-call | tf_op jit(solution)/shard_map/triangular_solve/custom-call.0 | solution.py:24
  629.6 3.9 fusion.197
  639.7 13.2 %custom-call.34 = f32[128,128]{1,0:T(8,128)} custom-call(f32[128,128]{1,0:T(8,128)} %broadcast_multiply_fusion.1), custom_call_target="Cholesky" | custom-call | tf_op jit(solution)/shard_map/cholesky/custom-call.1 | solution.py:30
  656.6 21.2 %custom-call.35 = f32[2,1,128,128]{2,3,1,0:T(8,128)} custom-call(f32[2,1,128,128]{3,2,1,0:T(8,128)} %fusion.141), custom_call_target="InvertDiagBlocksLowerTriangular" | custom-call | tf_op jit(solution)/shard_map/triangular_solve/custom-call.0 | solution.py:31
  715.1 3.1 fusion.15
  732.4 4.6 constant_dynamic-slice_fusion.4
  739.9 5.5 fusion.195
  746.2 6.9 fusion.27
  (331 shorter events, 211.4 us)
Async XLA Ops:
  7.2 732.8 %all-gather.2.cloned.1.call-start = ((), (), s32[]{:S(2)}) async-start(), calls=%async_computation | async-start | bytes 5242880 | tf_op jit(solution)/shard_map/all_gather | solution.py:75
  35.0 8.4 %copy-start.34 = (pred[8]{0:T(512)(128)(4,1)}, pred[8]{0:T(512)(128)(4,1)S(1)}, u32[]{:S(2)}) copy-start(pred[8]{0:T(512)(128)(4,1)S(1)} %get-tuple-element.123) | copy-start | bytes 28
  47.5 57.4 %copy-start.28 = (s32[4]{0:T(128)S(1)}, s32[4]{0:T(128)}, u32[]{:S(2)}) copy-start(s32[4]{0:T(128)} %param.19) | copy-start | bytes 52
  48.7 68.4 %copy-start.30 = (f32[1,4,256]{2,1,0:T(4,128)S(1)}, f32[1,4,256]{2,1,0:T(4,128)}, u32[]{:S(2)}) copy-start(f32[1,4,256]{2,1,0:T(4,128)} %param.18) | copy-start | bytes 12292
  48.7 68.4 %copy-start.31 = (f32[1,4,256]{2,1,0:T(4,128)S(1)}, f32[1,4,256]{2,1,0:T(4,128)}, u32[]{:S(2)}) copy-start(f32[1,4,256]{2,1,0:T(4,128)} %param.17) | copy-start | bytes 12292
  305.2 53.7 %copy-start.33 = (f32[128]{0:T(128)S(1)}, f32[128]{0:T(128)}, u32[]{:S(2)}) copy-start(f32[128]{0:T(128)} %get-tuple-element.70) | copy-start | bytes 1540
  340.0 18.9 %copy-start.20 = (f32[128,128]{1,0:T(8,128)}, f32[128,128]{1,0:T(8,128)S(1)}, u32[]{:S(2)}) copy-start(f32[128,128]{1,0:T(8,128)S(1)} %get-tuple-element.37) | copy-start | bytes 196612
  340.4 4.4 copy-start.7
  424.8 7.7 %copy-start.6 = (bf16[4,256,512]{2,1,0:T(8,128)(2,1)S(1)}, bf16[4,256,512]{2,1,0:T(8,128)(2,1)}, u32[]{:S(2)}) copy-start(bf16[4,256,512]{2,1,0:T(8,128)(2,1)} %slice.226) | copy-start | bytes 3145732
  429.1 28.8 %copy-start.32 = (f32[128]{0:T(128)S(1)}, f32[128]{0:T(128)}, u32[]{:S(2)}) copy-start(f32[128]{0:T(128)} %get-tuple-element.68) | copy-start | bytes 1540
  443.2 0.7 copy-start.14
  482.9 3.8 copy-start.9
  487.3 67.8 %copy-start.25 = (f32[1,512]{1,0:T(1,128)}, f32[1,512]{1,0:T(1,128)S(1)}, u32[]{:S(2)}) copy-start(f32[1,512]{1,0:T(1,128)S(1)} %broadcast.569) | copy-start | bytes 6148
  531.2 14.9 %copy-start.10 = (f32[2,128,128]{2,1,0:T(8,128)S(1)}, f32[2,128,128]{2,1,0:T(8,128)}, u32[]{:S(2)}) copy-start(f32[2,128,128]{2,1,0:T(8,128)} %copy-done.9) | copy-start | bytes 393220
  533.2 4.0 copy-start.21
  534.3 1.8 copy-start.18
  559.0 11.0 %copy-start = (bf16[8,256,512]{2,1,0:T(8,128)(2,1)S(1)}, bf16[8,256,512]{2,1,0:T(8,128)(2,1)}, u32[]{:S(2)}) copy-start(bf16[8,256,512]{2,1,0:T(8,128)(2,1)} %slice.238) | copy-start | bytes 6291460
  570.0 57.3 %copy-start.26 = (f32[1,512]{1,0:T(1,128)S(1)}, f32[1,512]{1,0:T(1,128)}, u32[]{:S(2)}) copy-start(f32[1,512]{1,0:T(1,128)} %fusion.302) | copy-start | bytes 6148
  570.0 57.9 %copy-start.27 = (f32[1,512]{1,0:T(1,128)S(1)}, f32[1,512]{1,0:T(1,128)}, u32[]{:S(2)}) copy-start(f32[1,512]{1,0:T(1,128)} %fusion.300) | copy-start | bytes 6148
  583.2 0.7 copy-start.13
  622.9 3.8 copy-start.8
  633.5 69.1 %copy-start.22 = (f32[512]{0:T(512)S(1)}, f32[512]{0:T(512)}, u32[]{:S(2)}) copy-start(f32[512]{0:T(512)} %add.349) | copy-start | bytes 6148
  633.5 69.2 %copy-start.23 = (f32[512]{0:T(512)S(1)}, f32[512]{0:T(512)}, u32[]{:S(2)}) copy-start(f32[512]{0:T(512)} %add.347) | copy-start | bytes 6148
  633.5 69.2 %copy-start.24 = (f32[512]{0:T(512)S(1)}, f32[512]{0:T(512)}, u32[]{:S(2)}) copy-start(f32[512]{0:T(512)} %add.348) | copy-start | bytes 6148
  679.9 4.2 copy-start.19
  680.9 3.2 copy-start.17
  705.4 15.6 %copy-start.5 = (f32[512,512]{1,0:T(8,128)S(1)}, f32[512,512]{1,0:T(8,128)}, u32[]{:S(2)}) copy-start(f32[512,512]{1,0:T(8,128)} %get-tuple-element.108) | copy-start | bytes 3145732
  709.5 14.4 %copy-start.2 = (f32[512,512]{1,0:T(8,128)S(1)}, f32[512,512]{1,0:T(8,128)}, u32[]{:S(2)}) copy-start(f32[512,512]{1,0:T(8,128)} %get-tuple-element.109) | copy-start | bytes 3145732
  712.3 14.5 %copy-start.3 = (f32[512,512]{1,0:T(8,128)S(1)}, f32[512,512]{1,0:T(8,128)}, u32[]{:S(2)}) copy-start(f32[512,512]{1,0:T(8,128)} %get-tuple-element.110) | copy-start | bytes 3145732
  715.1 14.5 %copy-start.4 = (f32[512,512]{1,0:T(8,128)S(1)}, f32[512,512]{1,0:T(8,128)}, u32[]{:S(2)}) copy-start(f32[512,512]{1,0:T(8,128)} %get-tuple-element.111) | copy-start | bytes 3145732
  732.4 13.1 %copy-start.29 = (pred[8]{0:T(512)(128)(4,1)S(1)}, pred[8]{0:T(512)(128)(4,1)}, u32[]{:S(2)}) copy-start(pred[8]{0:T(512)(128)(4,1)} %get-tuple-element.8) | copy-start | bytes 28
  732.4 13.8 %copy-start.1 = (bf16[1,4096,128]{2,1,0:T(8,128)(2,1)S(1)}, bf16[1,4096,128]{2,1,0:T(8,128)(2,1)}, u32[]{:S(2)}) copy-start(bf16[1,4096,128]{2,1,0:T(8,128)(2,1)} %param.12) | copy-start | bytes 3145732
  (4 other events, 2.7 us)
Sparse Core Ops, SparseCore 0:
  9.8 56.3 all-gather.1

commit v4 on v3

--- a/solution.py
+++ b/solution.py
@@ -59,6 +59,7 @@
     batch_order,
 ):
     highest = lax.Precision.HIGHEST
+    high = lax.Precision.HIGH
     batches = footprints.shape[0]
     slot_dev = footprints.shape[2]
     tile_cells = footprints.shape[4]
@@ -100,8 +101,8 @@
         live_tile = jnp.any((tile_ids[:, None] == local_ids[None, :]) & live_slot[:, None], axis=0)
         pattern = pattern + jnp.where(live_tile, 1 << position, 0)
     projected = jnp.concatenate(pieces, axis=0)
-    slotted = jnp.zeros((projected.shape[0], groups) + projected.shape[1:], jnp.float32)
-    slotted = lax.dynamic_update_index_in_dim(slotted, projected, me_member, 1)
+    own_group = (jnp.arange(groups, dtype=jnp.int32) == me_member)[None, :, None, None]
+    slotted = jnp.where(own_group, projected[:, None], 0.0)
     mean_parts = jnp.where(me_member == 0, jnp.stack(mean_parts), 0.0)
     summed, obs_means_base, values_all, errors_all = lax.psum(
         (slotted, mean_parts, jnp.stack(value_parts), jnp.stack(error_parts)),
@@ -116,9 +117,9 @@
         n_pat = 2**position
         part = summed[offset : offset + n_pat].astype(jnp.float32)
         offset += n_pat
-        obs_anoms = jnp.einsum("spm,smn->pn", part, jnp.stack(transforms), precision=highest)
-        obs_means = obs_means_base[position] + jnp.einsum(
-            "spm,sm->p", part, jnp.stack(shifts), precision=highest
+        obs_anoms = sum(jnp.dot(part[s], t, precision=high) for s, t in enumerate(transforms))
+        obs_means = obs_means_base[position] + sum(
+            jnp.dot(part[s], v, precision=high) for s, v in enumerate(shifts)
         )
         obs_round = obs_anoms.astype(jnp.bfloat16)
         transform, weights_obs = innovation(
@@ -126,11 +127,11 @@
         )
         wide_obs = obs_round.astype(jnp.float32)
         step = jnp.dot(
-            wide_obs.T, jnp.dot(transform, wide_obs, precision=highest), precision=highest
+            wide_obs.T, jnp.dot(transform, wide_obs, precision=high), precision=high
         ) / (members - 1)
-        lift = jnp.dot(wide_obs.T, weights_obs, precision=highest) / (members - 1)
-        new_transforms = [t - jnp.dot(t, step, precision=highest) for t in transforms]
-        new_shifts = [s + jnp.dot(t, lift, precision=highest) for t, s in zip(transforms, shifts)]
+        lift = jnp.dot(wide_obs.T, weights_obs, precision=high) / (members - 1)
+        new_transforms = [t - jnp.dot(t, step, precision=high) for t in transforms]
+        new_shifts = [s + jnp.dot(t, lift, precision=high) for t, s in zip(transforms, shifts)]
         transforms = transforms + new_transforms
         shifts = shifts + new_shifts
     own_cols = lax.dynamic_slice_in_dim(
@@ -139,10 +140,10 @@
     tile_transform = own_cols[pattern]
     tile_shift = jnp.stack(shifts)[pattern]
     wide_tiles = all_tiles.astype(jnp.float32)
-    updated = jnp.einsum("tcm,tmn->tcn", wide_tiles, tile_transform, precision=highest)
+    updated = jnp.einsum("tcm,tmn->tcn", wide_tiles, tile_transform, precision=high)
     touched = pattern > 0
     new_anoms = jnp.where(touched[:, None, None], updated.astype(jnp.bfloat16), tile_anoms)
-    shift_mean = jnp.einsum("tcm,tm->tc", wide_tiles, tile_shift, precision=highest)
+    shift_mean = jnp.einsum("tcm,tm->tc", wide_tiles, tile_shift, precision=high)
     new_means = jnp.where(touched[:, None], tile_means + shift_mean, tile_means)
     return (new_anoms.reshape(1, -1, member_dev), new_means.reshape(1, -1))
 

time: 771 us -> 679 us (0.88)
  local copies, waits for them, and re-layouts: 119 us -> 52.9 us
  matrix products: 152 us -> 127 us
    dynamic_update_slice x1 -> x0, local copies, waits for them, and re-layouts: 51.6 us -> none  [body(): slotted = lax.dynamic_update_index_in_dim(slotted, projected, me_member, 1)]
    dot_general x52 -> x74, matrix products: 99.9 us -> 76 us  [the longest x15 30.3 us: body(): new_transforms = [t - jnp.dot(t, step, precision=high) for t in transforms]]
    slice x7 -> x1, local copies, waits for them, and re-layouts: 13.4 us -> 3.64 us  [body(): part[s]]
  transfers between devices with their start and end apart: 1 -> 1, of which waited for: 0 -> 0; matrix products, arithmetic and copies ran while one was open for 75% -> 72% of each run, Pallas kernels for 0% -> 0%
where the time goes in v4:
time: 679 us; the launch traced here: 670 us
  other arithmetic  316 us (47%)
  blocking collectives  148 us (22%)
  matrix products  127 us (19%)
  local copies, waits for them, and re-layouts  52.9 us (8%)
  between operations  25.6 us (4%)
    psum x1, blocking collectives, body(): lax.psum((slotted, mean_parts, jnp.stack(value_parts), jnp.stack(error_pa...  148 us
    another operation x9, other arithmetic, innovation(): lax.linalg.triangular_solve(jnp.stack([factor_11, factor_11 + jnp.diag(er...  84.1 us
    another operation x8, other arithmetic, innovation(): lax.linalg.triangular_solve(jnp.stack([factor_22, factor_22 + jnp.diag(er...  83.9 us
    another operation x12, other arithmetic, innovation(): factor_22 = lax.linalg.cholesky(schur, symmetrize_input=True)  54.2 us
    another operation x12, other arithmetic, innovation(): lax.linalg.cholesky(innov_cov[:half, :half], symmetrize_input=False)  51.7 us
    dot_general x15, matrix products, body(): new_transforms = [t - jnp.dot(t, step, precision=high) for t in transforms]  30.3 us
  transfers between devices with their start and end apart: 1, of which 0 were waited for; matrix products, arithmetic and copies ran while one was open for 72% of the time, Pallas kernels for 0%

profile of v4, /device:TPU:1, one launch (start us, length us, event | category | flops | bytes accessed | tf_op | source)
XLA Modules:
  0.0 670.4 jit_solution(932925000148014732)
XLA Ops:
  48.1 4.1 broadcast_select_fusion
  55.5 2.1 convolution_bitcast_fusion
  57.7 2.2 convolution_bitcast_fusion.1
  59.9 2.2 convolution_bitcast_fusion.2
  62.2 2.2 convolution_bitcast_fusion.3
  64.4 148.1 %all-reduce.10 = (bf16[15,4,256,128]{2,3,1,0:T(8,128)(2,1)}, f32[4,256]{1,0:T(4,128)S(1)}, f32[4,256]{1,0:T(4,128)S(1)}, f32[4,256]{1,0:T(4,128)S(1)}) all-reduce(f32[15,4,256,128]{2,3,1,0:T(8,128)} %broadcast_select_fusion, ...), channel_id=1, replica_groups=mesh['space'=32,'member'=4,'lag'=2] {'space','member','lag'}, use_global_device_ids=true, to_apply=%region_8.9 | all-reduce | flops 1969152 | bytes 11821056 | tf_op jit(solution)/shard_map/psum | solution.py:107
  212.5 3.6 fusion.278
  217.9 11.7 %custom-call.20 = f32[128,128]{1,0:T(8,128)S(1)} custom-call(f32[128,128]{1,0:T(8,128)S(1)} %slice.367), custom_call_target="Cholesky" | custom-call | tf_op jit(solution)/shard_map/cholesky/custom-call.1 | solution.py:23
  231.0 19.8 %custom-call.21 = f32[2,1,128,128]{2,3,1,0:T(8,128)S(1)} custom-call(f32[2,1,128,128]{3,2,1,0:T(8,128)S(1)} %fusion.107), custom_call_target="InvertDiagBlocksLowerTriangular" | custom-call | tf_op jit(solution)/shard_map/triangular_solve/custom-call.0 | solution.py:24
  254.8 11.7 %custom-call.22 = f32[128,128]{1,0:T(8,128)S(1)} custom-call(f32[128,128]{1,0:T(8,128)S(1)} %fusion.133), custom_call_target="Cholesky" | custom-call | tf_op jit(solution)/shard_map/cholesky/custom-call.1 | solution.py:30
  267.9 19.9 %custom-call.23 = f32[2,1,128,128]{2,3,1,0:T(8,128)S(1)} custom-call(f32[2,1,128,128]{3,2,1,0:T(8,128)S(1)} %fusion.108), custom_call_target="InvertDiagBlocksLowerTriangular" | custom-call | tf_op jit(solution)/shard_map/triangular_solve/custom-call.0 | solution.py:31
  293.9 11.7 %custom-call.24 = f32[128,128]{1,0:T(8,128)S(1)} custom-call(f32[128,128]{1,0:T(8,128)S(1)} %slice.379), custom_call_target="Cholesky" | custom-call | tf_op jit(solution)/shard_map/cholesky/custom-call.1 | solution.py:23
  307.7 20.5 %custom-call.25 = f32[2,1,128,128]{2,3,1,0:T(8,128)} custom-call(f32[2,1,128,128]{3,2,1,0:T(8,128)S(1)} %fusion.109), custom_call_target="InvertDiagBlocksLowerTriangular" | custom-call | tf_op jit(solution)/shard_map/triangular_solve/custom-call.0 | solution.py:24
  335.2 11.7 %custom-call.26 = f32[128,128]{1,0:T(8,128)S(1)} custom-call(f32[128,128]{1,0:T(8,128)S(1)} %fusion.132), custom_call_target="Cholesky" | custom-call | tf_op jit(solution)/shard_map/cholesky/custom-call.1 | solution.py:30
  349.0 20.1 %custom-call.27 = f32[2,1,128,128]{2,3,1,0:T(8,128)S(1)} custom-call(f32[2,1,128,128]{3,2,1,0:T(8,128)S(1)} %fusion.110), custom_call_target="InvertDiagBlocksLowerTriangular" | custom-call | tf_op jit(solution)/shard_map/triangular_solve/custom-call.0 | solution.py:31
  388.8 12.5 %custom-call.28 = f32[128,128]{1,0:T(8,128)S(1)} custom-call(f32[128,128]{1,0:T(8,128)} %copy.235), custom_call_target="Cholesky" | custom-call | tf_op jit(solution)/shard_map/cholesky/custom-call.1 | solution.py:23
  404.4 21.3 %custom-call.29 = f32[2,1,128,128]{2,3,1,0:T(8,128)} custom-call(f32[2,1,128,128]{3,2,1,0:T(8,128)} %fusion.111), custom_call_target="InvertDiagBlocksLowerTriangular" | custom-call | tf_op jit(solution)/shard_map/triangular_solve/custom-call.0 | solution.py:24
  437.3 13.2 %custom-call.30 = f32[128,128]{1,0:T(8,128)} custom-call(f32[128,128]{1,0:T(8,128)} %fusion.131), custom_call_target="Cholesky" | custom-call | tf_op jit(solution)/shard_map/cholesky/custom-call.1 | solution.py:30
  454.2 21.3 %custom-call.31 = f32[2,1,128,128]{2,3,1,0:T(8,128)} custom-call(f32[2,1,128,128]{3,2,1,0:T(8,128)} %fusion.112), custom_call_target="InvertDiagBlocksLowerTriangular" | custom-call | tf_op jit(solution)/shard_map/triangular_solve/custom-call.0 | solution.py:31
  493.2 2.1 bitcast_dynamic-update-slice_fusion.2
  495.4 2.1 bitcast_dynamic-update-slice_fusion.1
  497.5 2.1 bitcast_dynamic-update-slice_fusion
  509.8 13.0 %custom-call.32 = f32[128,128]{1,0:T(8,128)S(1)} custom-call(f32[128,128]{1,0:T(8,128)} %copy.251), custom_call_target="Cholesky" | custom-call | tf_op jit(solution)/shard_map/cholesky/custom-call.1 | solution.py:23
  525.6 21.1 %custom-call.33 = f32[2,1,128,128]{2,3,1,0:T(8,128)} custom-call(f32[2,1,128,128]{3,2,1,0:T(8,128)} %fusion.113), custom_call_target="InvertDiagBlocksLowerTriangular" | custom-call | tf_op jit(solution)/shard_map/triangular_solve/custom-call.0 | solution.py:24
  565.8 13.2 %custom-call.34 = f32[128,128]{1,0:T(8,128)} custom-call(f32[128,128]{1,0:T(8,128)} %broadcast_multiply_fusion.1), custom_call_target="Cholesky" | custom-call | tf_op jit(solution)/shard_map/cholesky/custom-call.1 | solution.py:30
  582.9 21.2 %custom-call.35 = f32[2,1,128,128]{2,3,1,0:T(8,128)} custom-call(f32[2,1,128,128]{3,2,1,0:T(8,128)} %fusion.114), custom_call_target="InvertDiagBlocksLowerTriangular" | custom-call | tf_op jit(solution)/shard_map/triangular_solve/custom-call.0 | solution.py:31
  638.5 2.1 fusion.7
  644.8 2.3 fusion.13
  647.0 4.6 constant_dynamic-slice_fusion.4
  651.6 3.0 gather_fusion.8
  654.6 4.6 fusion.168
  659.9 3.4 fusion.15
  (370 shorter events, 190.0 us)
Async XLA Ops:
  7.2 20.5 %copy-start.3 = (bf16[1,4096,128]{2,1,0:T(8,128)(2,1)S(1)}, bf16[1,4096,128]{2,1,0:T(8,128)(2,1)}, u32[]{:S(2)}) copy-start(bf16[1,4096,128]{2,1,0:T(8,128)(2,1)} %param.12) | copy-start | bytes 3145732
  7.2 22.4 %copy-start.42 = (s32[4,1,1]{0,2,1:T(1,128)S(1)}, s32[4,1,1]{0,2,1:T(1,128)}, u32[]{:S(2)}) copy-start(s32[4,1,1]{0,2,1:T(1,128)} %param.16) | copy-start | bytes 52
  7.2 647.4 %all-gather.2.cloned.1.call-start = ((), (), s32[]{:S(2)}) async-start(), calls=%async_computation | async-start | bytes 5242880 | tf_op jit(solution)/shard_map/all_gather | solution.py:76
  33.0 8.4 %copy-start.47 = (pred[8]{0:T(512)(128)(4,1)}, pred[8]{0:T(512)(128)(4,1)S(1)}, u32[]{:S(2)}) copy-start(pred[8]{0:T(512)(128)(4,1)S(1)} %get-tuple-element.131) | copy-start | bytes 28
  52.2 12.1 %copy-start.45 = (f32[1,4,256]{2,1,0:T(4,128)S(1)}, f32[1,4,256]{2,1,0:T(4,128)}, u32[]{:S(2)}) copy-start(f32[1,4,256]{2,1,0:T(4,128)} %param.18) | copy-start | bytes 12292
  52.2 12.1 %copy-start.46 = (f32[1,4,256]{2,1,0:T(4,128)S(1)}, f32[1,4,256]{2,1,0:T(4,128)}, u32[]{:S(2)}) copy-start(f32[1,4,256]{2,1,0:T(4,128)} %param.17) | copy-start | bytes 12292
  216.2 162.8 %copy-start.18 = (bf16[1,256,4,128]{1,3,2,0:T(8,128)(2,1)}, bf16[1,256,4,128]{1,3,2,0:T(8,128)(2,1)S(1)}, u32[]{:S(2)}) copy-start(bf16[1,256,4,128]{1,3,2,0:T(8,128)(2,1)S(1)} %get-tuple-element.20) | copy-start | bytes 786436
  252.0 37.1 %copy-start.35 = (f32[128,128]{1,0:T(8,128)}, f32[128,128]{1,0:T(8,128)S(1)}, u32[]{:S(2)}) copy-start(f32[128,128]{1,0:T(8,128)S(1)} %get-tuple-element.40) | copy-start | bytes 196612
  267.9 23.9 %copy-start.21 = (bf16[1,256,4,128]{1,3,2,0:T(8,128)(2,1)S(1)}, bf16[1,256,4,128]{1,3,2,0:T(8,128)(2,1)}, u32[]{:S(2)}) copy-start(bf16[1,256,4,128]{1,3,2,0:T(8,128)(2,1)} %get-tuple-element.23) | copy-start | bytes 786436
  291.8 43.1 %copy-start.22 = (bf16[1,256,4,128]{1,3,2,0:T(8,128)(2,1)S(1)}, bf16[1,256,4,128]{1,3,2,0:T(8,128)(2,1)}, u32[]{:S(2)}) copy-start(bf16[1,256,4,128]{1,3,2,0:T(8,128)(2,1)} %get-tuple-element.23) | copy-start | bytes 786436
  293.8 77.5 %copy-start.28 = (bf16[1,256,4,128]{1,3,2,0:T(8,128)(2,1)S(1)}, bf16[1,256,4,128]{1,3,2,0:T(8,128)(2,1)}, u32[]{:S(2)}) copy-start(bf16[1,256,4,128]{1,3,2,0:T(8,128)(2,1)} %get-tuple-element.22) | copy-start | bytes 786436
  330.9 40.4 %copy-start.37 = (f32[128,128]{1,0:T(8,128)}, f32[128,128]{1,0:T(8,128)S(1)}, u32[]{:S(2)}) copy-start(f32[128,128]{1,0:T(8,128)S(1)} %get-tuple-element.36) | copy-start | bytes 196612
  335.1 37.9 %copy-start.38 = (f32[128,128]{1,0:T(8,128)S(1)}, f32[128,128]{1,0:T(8,128)}, u32[]{:S(2)}) copy-start(f32[128,128]{1,0:T(8,128)} %get-tuple-element.37) | copy-start | bytes 196612
  375.1 4.4 copy-start.20
  475.5 8.0 %copy-start.27 = (bf16[1,256,4,128]{1,3,2,0:T(8,128)(2,1)S(1)}, bf16[1,256,4,128]{1,3,2,0:T(8,128)(2,1)}, u32[]{:S(2)}) copy-start(bf16[1,256,4,128]{1,3,2,0:T(8,128)(2,1)} %get-tuple-element.18) | copy-start | bytes 786436
  475.5 9.1 %copy-start.25 = (f32[2,128,128]{2,1,0:T(8,128)S(1)}, f32[2,128,128]{2,1,0:T(8,128)}, u32[]{:S(2)}) copy-start(f32[2,128,128]{2,1,0:T(8,128)} %copy-done.24) | copy-start | bytes 393220
  475.5 10.6 %copy-start.17 = (bf16[1,256,4,128]{1,3,2,0:T(8,128)(2,1)S(1)}, bf16[1,256,4,128]{1,3,2,0:T(8,128)(2,1)}, u32[]{:S(2)}) copy-start(bf16[1,256,4,128]{1,3,2,0:T(8,128)(2,1)} %get-tuple-element.17) | copy-start | bytes 786436
  475.5 11.4 %copy-start.16 = (bf16[1,256,4,128]{1,3,2,0:T(8,128)(2,1)S(1)}, bf16[1,256,4,128]{1,3,2,0:T(8,128)(2,1)}, u32[]{:S(2)}) copy-start(bf16[1,256,4,128]{1,3,2,0:T(8,128)(2,1)} %get-tuple-element.16) | copy-start | bytes 786436
  475.6 12.1 %copy-start.15 = (bf16[1,256,4,128]{1,3,2,0:T(8,128)(2,1)S(1)}, bf16[1,256,4,128]{1,3,2,0:T(8,128)(2,1)}, u32[]{:S(2)}) copy-start(bf16[1,256,4,128]{1,3,2,0:T(8,128)(2,1)} %get-tuple-element.15) | copy-start | bytes 786436
  484.6 5.6 copy-start.39
  484.6 5.6 copy-start.40
  493.2 6.4 copy-start
  495.4 4.8 copy-start.5
  495.4 4.3 copy-start.14
  604.1 11.0 %copy-start.6 = (f32[512,512]{1,0:T(8,128)S(1)}, f32[512,512]{1,0:T(8,128)}, u32[]{:S(2)}) copy-start(f32[512,512]{1,0:T(8,128)} %copy-done.5) | copy-start | bytes 3145732
  632.3 6.2 copy-start.1
  634.3 6.3 copy-start.7
  636.4 6.3 copy-start.9
  638.5 6.3 copy-start.11
  651.6 7.6 %copy-start.44 = (pred[8]{0:T(512)(128)(4,1)S(1)}, pred[8]{0:T(512)(128)(4,1)}, u32[]{:S(2)}) copy-start(pred[8]{0:T(512)(128)(4,1)} %get-tuple-element.8) | copy-start | bytes 28
  651.6 8.3 %copy-start.4 = (bf16[1,4096,128]{2,1,0:T(8,128)(2,1)S(1)}, bf16[1,4096,128]{2,1,0:T(8,128)(2,1)}, u32[]{:S(2)}) copy-start(bf16[1,4096,128]{2,1,0:T(8,128)(2,1)} %param.12) | copy-start | bytes 3145732
  654.6 5.3 copy-start.2
  (17 other events, 37.0 us)
Sparse Core Ops, SparseCore 0:
  9.8 56.3 all-gather.1

commit v5 on v4

--- a/solution.py
+++ b/solution.py
@@ -117,10 +117,14 @@
         n_pat = 2**position
         part = summed[offset : offset + n_pat].astype(jnp.float32)
         offset += n_pat
-        obs_anoms = sum(jnp.dot(part[s], t, precision=high) for s, t in enumerate(transforms))
-        obs_means = obs_means_base[position] + sum(
-            jnp.dot(part[s], v, precision=high) for s, v in enumerate(shifts)
-        )
+        if position == 0:
+            obs_anoms = part[0]
+            obs_means = obs_means_base[position]
+        else:
+            obs_anoms = sum(jnp.dot(part[s], t, precision=high) for s, t in enumerate(transforms))
+            obs_means = obs_means_base[position] + sum(
+                jnp.dot(part[s], v, precision=high) for s, v in enumerate(shifts)
+            )
         obs_round = obs_anoms.astype(jnp.bfloat16)
         transform, weights_obs = innovation(
             obs_round, values_all[position], obs_means, errors_all[position], members
@@ -130,13 +134,24 @@
             wide_obs.T, jnp.dot(transform, wide_obs, precision=high), precision=high
         ) / (members - 1)
         lift = jnp.dot(wide_obs.T, weights_obs, precision=high) / (members - 1)
-        new_transforms = [t - jnp.dot(t, step, precision=high) for t in transforms]
-        new_shifts = [s + jnp.dot(t, lift, precision=high) for t, s in zip(transforms, shifts)]
-        transforms = transforms + new_transforms
-        shifts = shifts + new_shifts
-    own_cols = lax.dynamic_slice_in_dim(
-        jnp.stack(transforms), me_member * member_dev, member_dev, axis=2
-    )
+        if position == batches - 1:
+            own_step = lax.dynamic_slice_in_dim(step, me_member * member_dev, member_dev, axis=1)
+            own_cols = [
+                lax.dynamic_slice_in_dim(t, me_member * member_dev, member_dev, axis=1)
+                for t in transforms
+            ]
+            own_cols = own_cols + [
+                c - jnp.dot(t, own_step, precision=high) for t, c in zip(transforms, own_cols)
+            ]
+        elif position == 0:
+            transforms = transforms + [transforms[0] - step]
+        else:
+            transforms = transforms + [t - jnp.dot(t, step, precision=high) for t in transforms]
+        if position == 0:
+            shifts = shifts + [lift]
+        else:
+            shifts = shifts + [s + jnp.dot(t, lift, precision=high) for t, s in zip(transforms, shifts)]
+    own_cols = jnp.stack(own_cols)
     tile_transform = own_cols[pattern]
     tile_shift = jnp.stack(shifts)[pattern]
     wide_tiles = all_tiles.astype(jnp.float32)

time: 679 us -> 693 us (1.021)
  local copies, waits for them, and re-layouts: 52.9 us -> 71.6 us
    slice x1 -> x15, local copies, waits for them, and re-layouts: 3.64 us -> 21.3 us  [body(): part[s]]
    dot_general x15 -> x14, matrix products: 30.3 us -> 20 us  [the longest x8 10.2 us: body(): jnp.dot(t, own_step, precision=high)]
    unnamed x98 -> x122, local copies, waits for them, and re-layouts: 2.76 us -> 10.7 us
    dot_general x15 -> x14, matrix products: 13.4 us -> 16.6 us  [body(): jnp.dot(part[s], v, precision=high)]
  transfers between devices with their start and end apart: 1 -> 1, of which waited for: 0 -> 0; matrix products, arithmetic and copies ran while one was open for 72% -> 73% of each run, Pallas kernels for 0% -> 0%
where the time goes in v5:
time: 693 us; the launch traced here: 685 us
  other arithmetic  313 us (45%)
  blocking collectives  148 us (21%)
  matrix products  125 us (18%)
  local copies, waits for them, and re-layouts  71.6 us (10%)
  between operations  26 us (4%)
    psum x1, blocking collectives, body(): lax.psum((slotted, mean_parts, jnp.stack(value_parts), jnp.stack(error_pa...  148 us
    another operation x8, other arithmetic, innovation(): lax.linalg.triangular_solve(jnp.stack([factor_22, factor_22 + jnp.diag(er...  83.8 us
    another operation x9, other arithmetic, innovation(): lax.linalg.triangular_solve(jnp.stack([factor_11, factor_11 + jnp.diag(er...  83.8 us
    another operation x12, other arithmetic, innovation(): factor_22 = lax.linalg.cholesky(schur, symmetrize_input=True)  54.2 us
    another operation x12, other arithmetic, innovation(): lax.linalg.cholesky(innov_cov[:half, :half], symmetrize_input=False)  51.3 us
    slice x15, local copies, waits for them, and re-layouts, body(): part[s]  21.3 us
    dot_general x14, matrix products, body(): jnp.dot(part[s], v, precision=high)  16.6 us
  transfers between devices with their start and end apart: 1, of which 0 were waited for; matrix products, arithmetic and copies ran while one was open for 73% of the time, Pallas kernels for 0%

profile of v5, /device:TPU:1, one launch (start us, length us, event | category | flops | bytes accessed | tf_op | source)
XLA Modules:
  0.0 684.5 jit_solution(3048882474421963275)
XLA Ops:
  25.3 2.0 gather_fusion.3
  36.8 2.5 fusion.28
  45.8 4.2 broadcast_select_fusion
  53.4 2.1 convolution_bitcast_fusion.1
  55.6 2.2 convolution_bitcast_fusion.2
  57.8 2.2 convolution_bitcast_fusion.3
  60.1 2.2 convolution_bitcast_fusion.4
  62.4 147.9 %all-reduce.10 = (bf16[15,4,256,128]{3,2,1,0:T(8,128)(2,1)}, f32[4,256]{1,0:T(4,128)S(1)}, f32[4,256]{1,0:T(4,128)S(1)}, f32[4,256]{1,0:T(4,128)S(1)}) all-reduce(f32[15,4,256,128]{3,2,1,0:T(8,128)} %broadcast_select_fusion, ...), channel_id=1, replica_groups=mesh['space'=32,'member'=4,'lag'=2] {'space','member','lag'}, use_global_device_ids=true, to_apply=%region_8.9 | all-reduce | flops 1969152 | bytes 11821056 | tf_op jit(solution)/shard_map/psum | solution.py:107
  212.4 11.7 %custom-call.20 = f32[128,128]{1,0:T(8,128)S(1)} custom-call(f32[128,128]{1,0:T(8,128)S(1)} %slice.370), custom_call_target="Cholesky" | custom-call | tf_op jit(solution)/shard_map/cholesky/custom-call.1 | solution.py:23
  225.6 20.2 %custom-call.21 = f32[2,1,128,128]{2,3,1,0:T(8,128)S(1)} custom-call(f32[2,1,128,128]{3,2,1,0:T(8,128)S(1)} %fusion.108), custom_call_target="InvertDiagBlocksLowerTriangular" | custom-call | tf_op jit(solution)/shard_map/triangular_solve/custom-call.0 | solution.py:24
  247.0 3.7 fusion.293
  252.4 11.7 %custom-call.22 = f32[128,128]{1,0:T(8,128)S(1)} custom-call(f32[128,128]{1,0:T(8,128)S(1)} %fusion.134), custom_call_target="Cholesky" | custom-call | tf_op jit(solution)/shard_map/cholesky/custom-call.1 | solution.py:30
  265.6 19.8 %custom-call.23 = f32[2,1,128,128]{2,3,1,0:T(8,128)S(1)} custom-call(f32[2,1,128,128]{3,2,1,0:T(8,128)S(1)} %fusion.109), custom_call_target="InvertDiagBlocksLowerTriangular" | custom-call | tf_op jit(solution)/shard_map/triangular_solve/custom-call.0 | solution.py:31
  291.1 11.7 %custom-call.24 = f32[128,128]{1,0:T(8,128)S(1)} custom-call(f32[128,128]{1,0:T(8,128)S(1)} %slice.382), custom_call_target="Cholesky" | custom-call | tf_op jit(solution)/shard_map/cholesky/custom-call.1 | solution.py:23
  304.3 19.9 %custom-call.25 = f32[2,1,128,128]{2,3,1,0:T(8,128)S(1)} custom-call(f32[2,1,128,128]{3,2,1,0:T(8,128)S(1)} %fusion.110), custom_call_target="InvertDiagBlocksLowerTriangular" | custom-call | tf_op jit(solution)/shard_map/triangular_solve/custom-call.0 | solution.py:24
  327.0 11.7 %custom-call.26 = f32[128,128]{1,0:T(8,128)S(1)} custom-call(f32[128,128]{1,0:T(8,128)S(1)} %fusion.133), custom_call_target="Cholesky" | custom-call | tf_op jit(solution)/shard_map/cholesky/custom-call.1 | solution.py:30
  340.8 20.1 %custom-call.27 = f32[2,1,128,128]{2,3,1,0:T(8,128)S(1)} custom-call(f32[2,1,128,128]{3,2,1,0:T(8,128)S(1)} %fusion.111), custom_call_target="InvertDiagBlocksLowerTriangular" | custom-call | tf_op jit(solution)/shard_map/triangular_solve/custom-call.0 | solution.py:31
  384.5 12.5 %custom-call.28 = f32[128,128]{1,0:T(8,128)S(1)} custom-call(f32[128,128]{1,0:T(8,128)} %copy.190), custom_call_target="Cholesky" | custom-call | tf_op jit(solution)/shard_map/cholesky/custom-call.1 | solution.py:23
  400.0 21.3 %custom-call.29 = f32[2,1,128,128]{2,3,1,0:T(8,128)} custom-call(f32[2,1,128,128]{3,2,1,0:T(8,128)} %fusion.112), custom_call_target="InvertDiagBlocksLowerTriangular" | custom-call | tf_op jit(solution)/shard_map/triangular_solve/custom-call.0 | solution.py:24
  432.9 13.2 %custom-call.30 = f32[128,128]{1,0:T(8,128)} custom-call(f32[128,128]{1,0:T(8,128)} %fusion.132), custom_call_target="Cholesky" | custom-call | tf_op jit(solution)/shard_map/cholesky/custom-call.1 | solution.py:30
  449.8 21.3 %custom-call.31 = f32[2,1,128,128]{2,3,1,0:T(8,128)} custom-call(f32[2,1,128,128]{3,2,1,0:T(8,128)} %fusion.113), custom_call_target="InvertDiagBlocksLowerTriangular" | custom-call | tf_op jit(solution)/shard_map/triangular_solve/custom-call.0 | solution.py:31
  483.9 2.1 fusion.38
  492.1 2.1 convolution_subtract_fusion.2
  494.1 2.1 convolution_subtract_fusion.1
  496.2 2.1 convolution_subtract_fusion
  529.4 12.5 %custom-call.32 = f32[128,128]{1,0:T(8,128)S(1)} custom-call(f32[128,128]{1,0:T(8,128)} %copy.214), custom_call_target="Cholesky" | custom-call | tf_op jit(solution)/shard_map/cholesky/custom-call.1 | solution.py:23
  545.1 21.1 %custom-call.33 = f32[2,1,128,128]{2,3,1,0:T(8,128)} custom-call(f32[2,1,128,128]{3,2,1,0:T(8,128)} %fusion.114), custom_call_target="InvertDiagBlocksLowerTriangular" | custom-call | tf_op jit(solution)/shard_map/triangular_solve/custom-call.0 | solution.py:24
  586.0 13.2 %custom-call.34 = f32[128,128]{1,0:T(8,128)} custom-call(f32[128,128]{1,0:T(8,128)} %broadcast_multiply_fusion.1), custom_call_target="Cholesky" | custom-call | tf_op jit(solution)/shard_map/cholesky/custom-call.1 | solution.py:30
  603.1 21.2 %custom-call.35 = f32[2,1,128,128]{2,3,1,0:T(8,128)} custom-call(f32[2,1,128,128]{3,2,1,0:T(8,128)} %fusion.115), custom_call_target="InvertDiagBlocksLowerTriangular" | custom-call | tf_op jit(solution)/shard_map/triangular_solve/custom-call.0 | solution.py:31
  665.8 3.0 gather_fusion.8
  668.8 4.6 fusion.169
  674.1 3.4 fusion.1
  (402 shorter events, 207.3 us)
Async XLA Ops:
  7.2 20.7 %copy-start.10 = (bf16[1,4096,128]{2,1,0:T(8,128)(2,1)S(1)}, bf16[1,4096,128]{2,1,0:T(8,128)(2,1)}, u32[]{:S(2)}) copy-start(bf16[1,4096,128]{2,1,0:T(8,128)(2,1)} %param.12) | copy-start | bytes 3145732
  7.2 22.6 %copy-start.47 = (s32[4,1,1]{0,2,1:T(1,128)S(1)}, s32[4,1,1]{0,2,1:T(1,128)}, u32[]{:S(2)}) copy-start(s32[4,1,1]{0,2,1:T(1,128)} %param.16) | copy-start | bytes 52
  7.2 661.6 %all-gather.2.cloned.1.call-start = ((), (), s32[]{:S(2)}) async-start(), calls=%async_computation | async-start | bytes 5242880 | tf_op jit(solution)/shard_map/all_gather | solution.py:76
  33.2 9.1 %copy-start.54 = (pred[8]{0:T(512)(128)(4,1)}, pred[8]{0:T(512)(128)(4,1)S(1)}, u32[]{:S(2)}) copy-start(pred[8]{0:T(512)(128)(4,1)S(1)} %get-tuple-element.115) | copy-start | bytes 28
  50.1 12.2 %copy-start.50 = (f32[1,4,256]{2,1,0:T(4,128)S(1)}, f32[1,4,256]{2,1,0:T(4,128)}, u32[]{:S(2)}) copy-start(f32[1,4,256]{2,1,0:T(4,128)} %param.18) | copy-start | bytes 12292
  50.1 12.2 %copy-start.51 = (f32[1,4,256]{2,1,0:T(4,128)S(1)}, f32[1,4,256]{2,1,0:T(4,128)}, u32[]{:S(2)}) copy-start(f32[1,4,256]{2,1,0:T(4,128)} %param.17) | copy-start | bytes 12292
  246.9 41.7 %copy-start.39 = (f32[128,128]{1,0:T(8,128)}, f32[128,128]{1,0:T(8,128)S(1)}, u32[]{:S(2)}) copy-start(f32[128,128]{1,0:T(8,128)S(1)} %get-tuple-element.40) | copy-start | bytes 196612
  286.0 4.8 copy-start.35
  288.7 14.8 %copy-start.53 = (f32[128]{0:T(128)S(1)}, f32[128]{0:T(128)}, u32[]{:S(2)}) copy-start(f32[128]{0:T(128)} %get-tuple-element.69) | copy-start | bytes 1540
  289.5 35.8 %copy-start.55 = (f32[256,1]{0,1:T(1,128)S(1)}, f32[256,1]{0,1:T(1,128)}, u32[]{:S(2)}) copy-start(f32[256,1]{0,1:T(1,128)} %convolution_bitcast_fusion.12) | copy-start | bytes 3076
  290.6 71.0 %copy-start.52 = (f32[1,256]{1,0:T(1,128)S(1)}, f32[1,256]{1,0:T(1,128)}, u32[]{:S(2)}) copy-start(f32[1,256]{1,0:T(1,128)} %get-tuple-element.60) | copy-start | bytes 3076
  477.6 94.3 %copy-start.45 = (f32[1,512]{1,0:T(1,128)}, f32[1,512]{1,0:T(1,128)S(1)}, u32[]{:S(2)}) copy-start(f32[1,512]{1,0:T(1,128)S(1)} %fusion.36) | copy-start | bytes 6148
  500.7 11.3 %copy-start.16 = (bf16[1,256,4,128]{1,3,2,0:T(8,128)(2,1)}, bf16[1,256,4,128]{1,3,2,0:T(8,128)(2,1)S(1)}, u32[]{:S(2)}) copy-start(bf16[1,256,4,128]{1,3,2,0:T(8,128)(2,1)S(1)} %copy.203) | copy-start | bytes 786436
  513.1 6.8 copy-start.12
  515.0 4.4 copy-start.4
  515.0 4.4 copy-start.13
  624.3 11.0 %copy-start.5 = (f32[512,512]{1,0:T(8,128)S(1)}, f32[512,512]{1,0:T(8,128)}, u32[]{:S(2)}) copy-start(f32[512,512]{1,0:T(8,128)} %convolution_subtract_fusion.2) | copy-start | bytes 3145732
  624.4 16.1 %copy-start.46 = (f32[1,512]{1,0:T(1,128)S(1)}, f32[1,512]{1,0:T(1,128)}, u32[]{:S(2)}) copy-start(f32[1,512]{1,0:T(1,128)} %copy-done.45) | copy-start | bytes 6148
  645.6 6.6 copy-start.3
  645.6 7.3 %copy-start.1 = (f32[512,512]{1,0:T(8,128)S(1)}, f32[512,512]{1,0:T(8,128)}, u32[]{:S(2)}) copy-start(f32[512,512]{1,0:T(8,128)} %convolution_subtract_fusion) | copy-start | bytes 3145732
  645.7 8.1 %copy-start.23 = (f32[2,128,128]{2,1,0:T(8,128)S(1)}, f32[2,128,128]{2,1,0:T(8,128)}, u32[]{:S(2)}) copy-start(f32[2,128,128]{2,1,0:T(8,128)} %copy-done.22) | copy-start | bytes 393220
  645.7 8.3 %copy-start.26 = (f32[2,128,128]{2,1,0:T(8,128)S(1)}, f32[2,128,128]{2,1,0:T(8,128)}, u32[]{:S(2)}) copy-start(f32[2,128,128]{2,1,0:T(8,128)} %copy-done.25) | copy-start | bytes 393220
  645.7 8.5 %copy-start.34 = (f32[128,128]{1,0:T(8,128)S(1)}, f32[128,128]{1,0:T(8,128)}, u32[]{:S(2)}) copy-start(f32[128,128]{1,0:T(8,128)} %copy-done.33) | copy-start | bytes 196612
  645.7 8.5 %copy-start.37 = (f32[128,128]{1,0:T(8,128)S(1)}, f32[128,128]{1,0:T(8,128)}, u32[]{:S(2)}) copy-start(f32[128,128]{1,0:T(8,128)} %get-tuple-element.28) | copy-start | bytes 196612
  645.7 8.5 %copy-start.38 = (f32[128,128]{1,0:T(8,128)S(1)}, f32[128,128]{1,0:T(8,128)}, u32[]{:S(2)}) copy-start(f32[128,128]{1,0:T(8,128)} %get-tuple-element.29) | copy-start | bytes 196612
  645.7 8.5 %copy-start.41 = (f32[128,128]{1,0:T(8,128)S(1)}, f32[128,128]{1,0:T(8,128)}, u32[]{:S(2)}) copy-start(f32[128,128]{1,0:T(8,128)} %copy-done.40) | copy-start | bytes 196612
  645.7 8.5 %copy-start.42 = (f32[128,128]{1,0:T(8,128)S(1)}, f32[128,128]{1,0:T(8,128)}, u32[]{:S(2)}) copy-start(f32[128,128]{1,0:T(8,128)} %get-tuple-element.27) | copy-start | bytes 196612
  654.7 5.9 copy-start.8
  655.0 6.9 %copy-start.6 = (f32[512,512]{1,0:T(8,128)S(1)}, f32[512,512]{1,0:T(8,128)}, u32[]{:S(2)}) copy-start(f32[512,512]{1,0:T(8,128)} %convolution_subtract_fusion.2) | copy-start | bytes 3145732
  665.8 7.6 %copy-start.49 = (pred[8]{0:T(512)(128)(4,1)S(1)}, pred[8]{0:T(512)(128)(4,1)}, u32[]{:S(2)}) copy-start(pred[8]{0:T(512)(128)(4,1)} %get-tuple-element.8) | copy-start | bytes 28
  665.8 8.3 %copy-start.11 = (bf16[1,4096,128]{2,1,0:T(8,128)(2,1)S(1)}, bf16[1,4096,128]{2,1,0:T(8,128)(2,1)}, u32[]{:S(2)}) copy-start(bf16[1,4096,128]{2,1,0:T(8,128)(2,1)} %param.12) | copy-start | bytes 3145732
  668.8 5.3 copy-start.9
  (25 other events, 66.0 us)
Sparse Core Ops, SparseCore 0:
  9.8 56.3 all-gather.1

commit v6 on v4

--- a/solution.py
+++ b/solution.py
@@ -117,10 +117,14 @@
         n_pat = 2**position
         part = summed[offset : offset + n_pat].astype(jnp.float32)
         offset += n_pat
-        obs_anoms = sum(jnp.dot(part[s], t, precision=high) for s, t in enumerate(transforms))
-        obs_means = obs_means_base[position] + sum(
-            jnp.dot(part[s], v, precision=high) for s, v in enumerate(shifts)
-        )
+        if position == 0:
+            obs_anoms = part[0]
+            obs_means = obs_means_base[position]
+        else:
+            obs_anoms = sum(jnp.dot(part[s], t, precision=high) for s, t in enumerate(transforms))
+            obs_means = obs_means_base[position] + sum(
+                jnp.dot(part[s], v, precision=high) for s, v in enumerate(shifts)
+            )
         obs_round = obs_anoms.astype(jnp.bfloat16)
         transform, weights_obs = innovation(
             obs_round, values_all[position], obs_means, errors_all[position], members

time: 679 us -> 707 us (1.041)
  local copies, waits for them, and re-layouts: 52.9 us -> 69.6 us
  matrix products: 127 us -> 141 us
    slice x1 -> x15, local copies, waits for them, and re-layouts: 3.64 us -> 19.6 us  [body(): part[s]]
    dot_general x15 -> x14, matrix products: 13.4 us -> 17.1 us  [body(): jnp.dot(part[s], v, precision=high)]
  transfers between devices with their start and end apart: 1 -> 1, of which waited for: 0 -> 0; matrix products, arithmetic and copies ran while one was open for 72% -> 73% of each run, Pallas kernels for 0% -> 0%
where the time goes in v6:
time: 707 us; the launch traced here: 698 us
  other arithmetic  313 us (44%)
  blocking collectives  148 us (21%)
  matrix products  141 us (20%)
  local copies, waits for them, and re-layouts  69.6 us (10%)
  between operations  25.8 us (4%)
    psum x1, blocking collectives, body(): lax.psum((slotted, mean_parts, jnp.stack(value_parts), jnp.stack(error_pa...  148 us
    another operation x8, other arithmetic, innovation(): lax.linalg.triangular_solve(jnp.stack([factor_22, factor_22 + jnp.diag(er...  83.9 us
    another operation x9, other arithmetic, innovation(): lax.linalg.triangular_solve(jnp.stack([factor_11, factor_11 + jnp.diag(er...  83.5 us
    another operation x12, other arithmetic, innovation(): factor_22 = lax.linalg.cholesky(schur, symmetrize_input=True)  54.2 us
    another operation x12, other arithmetic, innovation(): lax.linalg.cholesky(innov_cov[:half, :half], symmetrize_input=False)  51.2 us
    dot_general x15, matrix products, body(): new_transforms = [t - jnp.dot(t, step, precision=high) for t in transforms]  30.2 us
    slice x15, local copies, waits for them, and re-layouts, body(): part[s]  19.6 us
    dot_general x14, matrix products, body(): jnp.dot(part[s], v, precision=high)  17.1 us
  transfers between devices with their start and end apart: 1, of which 0 were waited for; matrix products, arithmetic and copies ran while one was open for 73% of the time, Pallas kernels for 0%

profile of v6, /device:TPU:1, one launch (start us, length us, event | category | flops | bytes accessed | tf_op | source)
XLA Modules:
  0.0 697.8 jit_solution(16536751715794307732)
XLA Ops:
  37.0 2.5 fusion.27
  46.0 4.2 broadcast_select_fusion
  53.6 2.1 convolution_bitcast_fusion.1
  55.8 2.2 convolution_bitcast_fusion.2
  58.0 2.2 convolution_bitcast_fusion.3
  60.3 2.2 convolution_bitcast_fusion.4
  62.5 148.0 %all-reduce.10 = (bf16[15,4,256,128]{3,2,1,0:T(8,128)(2,1)}, f32[4,256]{1,0:T(4,128)S(1)}, f32[4,256]{1,0:T(4,128)S(1)}, f32[4,256]{1,0:T(4,128)S(1)}) all-reduce(f32[15,4,256,128]{3,2,1,0:T(8,128)} %broadcast_select_fusion, ...), channel_id=1, replica_groups=mesh['space'=32,'member'=4,'lag'=2] {'space','member','lag'}, use_global_device_ids=true, to_apply=%region_8.9 | all-reduce | flops 1969152 | bytes 11821056 | tf_op jit(solution)/shard_map/psum | solution.py:107
  212.8 11.7 %custom-call.20 = f32[128,128]{1,0:T(8,128)S(1)} custom-call(f32[128,128]{1,0:T(8,128)S(1)} %slice.370), custom_call_target="Cholesky" | custom-call | tf_op jit(solution)/shard_map/cholesky/custom-call.1 | solution.py:23
  225.9 19.8 %custom-call.21 = f32[2,1,128,128]{2,3,1,0:T(8,128)S(1)} custom-call(f32[2,1,128,128]{3,2,1,0:T(8,128)S(1)} %fusion.107), custom_call_target="InvertDiagBlocksLowerTriangular" | custom-call | tf_op jit(solution)/shard_map/triangular_solve/custom-call.0 | solution.py:24
  247.0 3.5 fusion.279
  253.3 11.7 %custom-call.22 = f32[128,128]{1,0:T(8,128)S(1)} custom-call(f32[128,128]{1,0:T(8,128)S(1)} %fusion.133), custom_call_target="Cholesky" | custom-call | tf_op jit(solution)/shard_map/cholesky/custom-call.1 | solution.py:30
  266.4 19.9 %custom-call.23 = f32[2,1,128,128]{2,3,1,0:T(8,128)S(1)} custom-call(f32[2,1,128,128]{3,2,1,0:T(8,128)S(1)} %fusion.108), custom_call_target="InvertDiagBlocksLowerTriangular" | custom-call | tf_op jit(solution)/shard_map/triangular_solve/custom-call.0 | solution.py:31
  296.1 11.7 %custom-call.24 = f32[128,128]{1,0:T(8,128)S(1)} custom-call(f32[128,128]{1,0:T(8,128)S(1)} %slice.382), custom_call_target="Cholesky" | custom-call | tf_op jit(solution)/shard_map/cholesky/custom-call.1 | solution.py:23
  309.9 19.9 %custom-call.25 = f32[2,1,128,128]{2,3,1,0:T(8,128)S(1)} custom-call(f32[2,1,128,128]{3,2,1,0:T(8,128)S(1)} %fusion.109), custom_call_target="InvertDiagBlocksLowerTriangular" | custom-call | tf_op jit(solution)/shard_map/triangular_solve/custom-call.0 | solution.py:24
  335.2 11.7 %custom-call.26 = f32[128,128]{1,0:T(8,128)S(1)} custom-call(f32[128,128]{1,0:T(8,128)S(1)} %fusion.132), custom_call_target="Cholesky" | custom-call | tf_op jit(solution)/shard_map/cholesky/custom-call.1 | solution.py:30
  348.4 20.1 %custom-call.27 = f32[2,1,128,128]{2,3,1,0:T(8,128)S(1)} custom-call(f32[2,1,128,128]{3,2,1,0:T(8,128)S(1)} %fusion.110), custom_call_target="InvertDiagBlocksLowerTriangular" | custom-call | tf_op jit(solution)/shard_map/triangular_solve/custom-call.0 | solution.py:31
  380.2 2.1 bitcast_dynamic-update-slice_fusion.4
  392.1 12.5 %custom-call.28 = f32[128,128]{1,0:T(8,128)S(1)} custom-call(f32[128,128]{1,0:T(8,128)} %copy.190), custom_call_target="Cholesky" | custom-call | tf_op jit(solution)/shard_map/cholesky/custom-call.1 | solution.py:23
  407.6 21.2 %custom-call.29 = f32[2,1,128,128]{2,3,1,0:T(8,128)} custom-call(f32[2,1,128,128]{3,2,1,0:T(8,128)} %fusion.111), custom_call_target="InvertDiagBlocksLowerTriangular" | custom-call | tf_op jit(solution)/shard_map/triangular_solve/custom-call.0 | solution.py:24
  440.5 13.2 %custom-call.30 = f32[128,128]{1,0:T(8,128)} custom-call(f32[128,128]{1,0:T(8,128)} %fusion.131), custom_call_target="Cholesky" | custom-call | tf_op jit(solution)/shard_map/cholesky/custom-call.1 | solution.py:30
  457.4 21.3 %custom-call.31 = f32[2,1,128,128]{2,3,1,0:T(8,128)} custom-call(f32[2,1,128,128]{3,2,1,0:T(8,128)} %fusion.112), custom_call_target="InvertDiagBlocksLowerTriangular" | custom-call | tf_op jit(solution)/shard_map/triangular_solve/custom-call.0 | solution.py:31
  520.8 2.1 bitcast_dynamic-update-slice_fusion.2
  525.0 2.2 bitcast_dynamic-update-slice_fusion
  537.8 12.5 %custom-call.32 = f32[128,128]{1,0:T(8,128)S(1)} custom-call(f32[128,128]{1,0:T(8,128)} %copy.214), custom_call_target="Cholesky" | custom-call | tf_op jit(solution)/shard_map/cholesky/custom-call.1 | solution.py:23
  553.1 21.1 %custom-call.33 = f32[2,1,128,128]{2,3,1,0:T(8,128)} custom-call(f32[2,1,128,128]{3,2,1,0:T(8,128)} %fusion.113), custom_call_target="InvertDiagBlocksLowerTriangular" | custom-call | tf_op jit(solution)/shard_map/triangular_solve/custom-call.0 | solution.py:24
  593.4 13.2 %custom-call.34 = f32[128,128]{1,0:T(8,128)} custom-call(f32[128,128]{1,0:T(8,128)} %broadcast_multiply_fusion.1), custom_call_target="Cholesky" | custom-call | tf_op jit(solution)/shard_map/cholesky/custom-call.1 | solution.py:30
  610.4 21.2 %custom-call.35 = f32[2,1,128,128]{2,3,1,0:T(8,128)} custom-call(f32[2,1,128,128]{3,2,1,0:T(8,128)} %fusion.114), custom_call_target="InvertDiagBlocksLowerTriangular" | custom-call | tf_op jit(solution)/shard_map/triangular_solve/custom-call.0 | solution.py:31
  672.2 2.3 fusion.13
  674.5 4.6 constant_dynamic-slice_fusion.4
  679.1 3.0 gather_fusion.8
  682.1 4.6 fusion.168
  687.4 3.4 fusion.15
  (393 shorter events, 218.0 us)
Async XLA Ops:
  7.2 20.7 %copy-start.3 = (bf16[1,4096,128]{2,1,0:T(8,128)(2,1)S(1)}, bf16[1,4096,128]{2,1,0:T(8,128)(2,1)}, u32[]{:S(2)}) copy-start(bf16[1,4096,128]{2,1,0:T(8,128)(2,1)} %param.12) | copy-start | bytes 3145732
  7.2 22.7 %copy-start.46 = (s32[4,1,1]{0,2,1:T(1,128)S(1)}, s32[4,1,1]{0,2,1:T(1,128)}, u32[]{:S(2)}) copy-start(s32[4,1,1]{0,2,1:T(1,128)} %param.16) | copy-start | bytes 52
  7.2 674.9 %all-gather.2.cloned.1.call-start = ((), (), s32[]{:S(2)}) async-start(), calls=%async_computation | async-start | bytes 5242880 | tf_op jit(solution)/shard_map/all_gather | solution.py:76
  33.3 9.2 %copy-start.53 = (pred[8]{0:T(512)(128)(4,1)}, pred[8]{0:T(512)(128)(4,1)S(1)}, u32[]{:S(2)}) copy-start(pred[8]{0:T(512)(128)(4,1)S(1)} %get-tuple-element.129) | copy-start | bytes 28
  39.5 4.1 copy-start.19
  46.0 4.2 copy-start.47
  50.2 12.2 %copy-start.49 = (f32[1,4,256]{2,1,0:T(4,128)S(1)}, f32[1,4,256]{2,1,0:T(4,128)}, u32[]{:S(2)}) copy-start(f32[1,4,256]{2,1,0:T(4,128)} %param.18) | copy-start | bytes 12292
  50.2 12.2 %copy-start.50 = (f32[1,4,256]{2,1,0:T(4,128)S(1)}, f32[1,4,256]{2,1,0:T(4,128)}, u32[]{:S(2)}) copy-start(f32[1,4,256]{2,1,0:T(4,128)} %param.17) | copy-start | bytes 12292
  210.6 76.7 %copy-start.51 = (f32[4,256]{1,0:T(4,128)}, f32[4,256]{1,0:T(4,128)S(1)}, u32[]{:S(2)}) copy-start(f32[4,256]{1,0:T(4,128)S(1)} %get-tuple-element.7) | copy-start | bytes 12292
  247.0 43.3 %copy-start.36 = (f32[128,128]{1,0:T(8,128)}, f32[128,128]{1,0:T(8,128)S(1)}, u32[]{:S(2)}) copy-start(f32[128,128]{1,0:T(8,128)S(1)} %get-tuple-element.40) | copy-start | bytes 196612
  286.7 4.4 copy-start.41
  286.9 6.4 copy-start.32
  293.3 54.3 %copy-start.52 = (f32[128]{0:T(128)S(1)}, f32[128]{0:T(128)}, u32[]{:S(2)}) copy-start(f32[128]{0:T(128)} %get-tuple-element.68) | copy-start | bytes 1540
  333.3 40.1 %copy-start.40 = (f32[128,128]{1,0:T(8,128)}, f32[128,128]{1,0:T(8,128)S(1)}, u32[]{:S(2)}) copy-start(f32[128,128]{1,0:T(8,128)S(1)} %get-tuple-element.36) | copy-start | bytes 196612
  369.6 6.4 copy-start.45
  369.8 6.2 copy-start.35
  373.5 8.8 %copy-start.15 = (bf16[1,256,4,128]{1,3,2,0:T(8,128)(2,1)}, bf16[1,256,4,128]{1,3,2,0:T(8,128)(2,1)S(1)}, u32[]{:S(2)}) copy-start(bf16[1,256,4,128]{1,3,2,0:T(8,128)(2,1)S(1)} %copy.183) | copy-start | bytes 786436
  378.4 4.4 copy-start.18
  480.7 4.0 copy-start.42
  510.0 7.4 %copy-start.28 = (f32[128,128]{1,0:T(8,128)S(1)}, f32[128,128]{1,0:T(8,128)}, u32[]{:S(2)}) copy-start(f32[128,128]{1,0:T(8,128)} %fusion.272) | copy-start | bytes 196612
  520.8 6.5 copy-start
  522.9 4.8 copy-start.5
  522.9 4.3 copy-start.14
  631.6 11.0 %copy-start.6 = (f32[512,512]{1,0:T(8,128)S(1)}, f32[512,512]{1,0:T(8,128)}, u32[]{:S(2)}) copy-start(f32[512,512]{1,0:T(8,128)} %copy-done.5) | copy-start | bytes 3145732
  633.7 4.3 copy-start.39
  659.8 6.2 copy-start.1
  661.9 6.3 copy-start.7
  663.9 6.2 copy-start.9
  666.0 6.2 copy-start.11
  679.1 7.6 %copy-start.48 = (pred[8]{0:T(512)(128)(4,1)S(1)}, pred[8]{0:T(512)(128)(4,1)}, u32[]{:S(2)}) copy-start(pred[8]{0:T(512)(128)(4,1)} %get-tuple-element.8) | copy-start | bytes 28
  679.1 8.3 %copy-start.4 = (bf16[1,4096,128]{2,1,0:T(8,128)(2,1)S(1)}, bf16[1,4096,128]{2,1,0:T(8,128)(2,1)}, u32[]{:S(2)}) copy-start(bf16[1,4096,128]{2,1,0:T(8,128)(2,1)} %param.12) | copy-start | bytes 3145732
  682.1 5.3 copy-start.2
  (23 other events, 56.8 us)
Sparse Core Ops, SparseCore 0:
  9.8 56.3 all-gather.1
